TPU v7x, 512 devices: a whole 4x4x16 slice. The times are simulated.
512 devices in a mesh: ops: 16 (over x, y), sec: 32 (over z, core).
Axes of the slice: x: 4, y: 4, z: 16, core: 2. Of those that a mesh axis runs over, the one named last changes fastest.
Arguments:
- wave: bfloat16 [32, 768, 768], P('sec')
- left_ops: bfloat16 [16, 32, 768, 768], P('ops', 'sec'), may hold values from -0.21875 to 0.21875
- right_ops: bfloat16 [16, 32, 768, 768], P('ops', 'sec'), may hold values from -0.21875 to 0.21875
- priors: bfloat16 [8, 32, 768, 768], P(None, 'sec', 'ops'), as said below
- row_sizes: int32 [32], P('sec'), may hold values from 64 to 768, as said below
- col_sizes: int32 [32], P('sec'), may hold values from 64 to 768, as said below
Outputs:
- sigma: bfloat16 [32, 768, 768], P('sec', 'ops')
- new_dir: bfloat16 [32, 768, 768], P('sec', 'ops')
- correlations: float32 [8], replicated
Inputs may be any that keep to these rules, and one draw needn't show every extreme that they name: `row_sizes`: one sector's block uses all 768 rows. `col_sizes`: one sector's block uses all 768 columns. `priors`: each prior vector has a norm of about one over all cells.
All inputs are finite; a program needn't handle non-finite values.
Results may differ from a plain program's by a relative error of at most 0.012.
Values sent between devices are 32-bit elements; how exact they have to be, the bound alone decides.
No kernel may reach another device: no remote copies, remote signals or barrier semaphores. Data moves between devices by JAX's collectives and lax.ppermute only.
A program may use at most 64 MiB of HBM per device.

v0:
```python
import jax
import jax.numpy as jnp
from jax import lax
from jax.sharding import PartitionSpec as P


def shards(wave, left_ops, right_ops, priors, row_sizes, col_sizes):
    width = wave.shape[1]
    sec_local = wave.shape[0]
    shard_rows = width // lax.axis_size("ops")
    first_row = lax.axis_index("ops") * shard_rows
    place = jnp.arange(width, dtype=jnp.int32)
    row_mask = (place[None, :] < row_sizes[:, None]).astype(jnp.float32)
    col_mask = (place[None, :] < col_sizes[:, None]).astype(jnp.float32)
    full_mask = row_mask[:, :, None] * col_mask[:, None, :]
    masked = wave * full_mask.astype(jnp.bfloat16)
    inner = jnp.einsum(
        "sab,ksjb->ksaj", masked, right_ops, preferred_element_type=jnp.float32
    ).astype(jnp.bfloat16)
    partial_all = jnp.einsum("ksia,ksaj->sij", left_ops, inner, preferred_element_type=jnp.float32)
    whole = lax.psum(partial_all, "ops")
    summed = lax.dynamic_slice_in_dim(whole, first_row, shard_rows, 1)
    mine_rows = lax.dynamic_slice_in_dim(row_mask, first_row, shard_rows, 1)
    mine_mask = mine_rows[:, :, None] * col_mask[:, None, :]
    sigma = (summed * mine_mask).astype(jnp.bfloat16)
    pmask = (priors * mine_mask[None].astype(jnp.bfloat16)).astype(jnp.float32)
    sig32 = sigma.astype(jnp.float32)
    local_over = jnp.einsum("psab,sab->p", pmask, sig32, precision=lax.Precision.HIGHEST)
    correlations = lax.psum(local_over, ("ops", "sec"))
    resid = sig32 - jnp.einsum("p,psab->sab", correlations, pmask, precision=lax.Precision.HIGHEST)
    total = lax.psum(jnp.sum(resid * resid), ("ops", "sec"))
    cells = sec_local * lax.axis_size("sec") * width * width
    new_dir = (resid / jnp.sqrt(total / cells + 1e-06)).astype(jnp.bfloat16)
    return (sigma, new_dir, correlations)


def solution(mesh):
    in_specs = (
        P("sec", None, None),
        P("ops", "sec", None, None),
        P("ops", "sec", None, None),
        P(None, "sec", "ops", None),
        P("sec"),
        P("sec"),
    )
    out_specs = (P("sec", "ops", None), P("sec", "ops", None), P())
    return jax.shard_map(shards, mesh=mesh, in_specs=in_specs, out_specs=out_specs, check_vma=False)
```

profile of v0, /device:TPU:1, one launch (start us, length us, event | category | flops | bytes accessed | tf_op | source)
XLA Modules:
  0.0 362.4 jit_solution(13174631265643082113)
XLA Ops:
  7.2 0.0 copy-start
  7.2 0.0 all-reduce.2.cloned.1.call-start
  8.6 0.0 copy-done
  8.6 5.6 %convolution_bitcast_fusion = f32[1,768,768]{1,2,0:T(8,128)} fusion(bf16[1,1,768,768]{3,2,1,0:T(8,128)(2,1)S(1)} %copy-done, bf16[1,768,768]{2,1,0:T(8,128)(2,1)} %param.6, bf16[1,1,768,768]{3,2,1,0:T(8,128)(2,1)} %param.8, f32[768]{0:T(1024)S(1)} %get-tuple-element.7, f32[768]{0:T(1024)S(1)} %get-tuple-element.6), kind=kOutput, calls=%fused_computation.1 | convolution fusion | flops 1814298624 | bytes 5904384 | tf_op jit(solution)/shard_map/ksia,ksaj->sij/dot_general | solution.py:20
  14.2 0.0 copy-start.1
  14.2 0.0 all-reduce.2.cloned.1.call-update
  14.2 0.1 multiply_convert_fusion.2
  14.3 0.9 copy-done.1
  15.3 125.8 %all-reduce.2.cloned.1.call-done = f32[1,768,768]{1,2,0:T(8,128)} async-done(((f32[1,768,768]{1,2,0:T(8,128)}), f32[1,768,768]{1,2,0:T(8,128)}) %all-reduce.2.cloned.1.call-update) | async-done | bytes 2359312 | tf_op jit(solution)/shard_map/psum | solution.py:21
  141.1 1.4 fusion.19
  142.5 0.2 copy.12
  142.7 0.5 convolution_bitcast_fusion.1
  143.2 105.0 %psum.22 = f32[8]{0:T(128)S(1)} all-reduce(f32[8]{0:T(128)S(1)} %convolution_bitcast_fusion.1), channel_id=1, replica_groups=mesh['ops'=16,'sec'=32] {'ops','sec'}, use_global_device_ids=true, to_apply=%region_1.0 | all-reduce | flops 8 | bytes 64 | tf_op jit(solution)/shard_map/psum | solution.py:29
  248.2 0.0 copy-start.2
  248.2 0.6 fusion.11
  248.8 0.2 copy.13
  249.0 1.4 multiply_convert_fusion.1
  250.4 2.0 multiply_reduce_fusion
  252.4 0.0 copy-done.2
  252.4 0.8 copy.9
  253.2 99.5 %psum.23 = f32[]{:T(128)} all-reduce(f32[]{:T(128)} %multiply_reduce_fusion), channel_id=1, replica_groups=mesh['ops'=16,'sec'=32] {'ops','sec'}, use_global_device_ids=true, to_apply=%region_3.0 | all-reduce | flops 1 | bytes 8 | tf_op jit(solution)/shard_map/psum | solution.py:31
  353.4 1.4 divide_convert_fusion
  354.8 0.8 copy.10
  (3 shorter events, 0.1 us)
Async XLA Ops:
  7.2 1.5 copy-start
  7.2 133.9 %all-reduce.2.cloned.1.call-start = ((), (), s32[]{:S(2)}) async-start(), calls=%async_computation | async-start | bytes 4718592 | tf_op jit(solution)/shard_map/psum | solution.py:21
  14.2 1.1 copy-start.1
  248.2 4.3 %copy-start.2 = (f32[8]{0:T(128)}, f32[8]{0:T(128)S(1)}, u32[]{:S(2)}) copy-start(f32[8]{0:T(128)S(1)} %psum.22) | copy-start | bytes 100
Sparse Core Ops, SparseCore 0:
  14.3 126.6 all-reduce.1
where the time goes:
time: 363 us; the launch traced here: 362 us
  blocking collectives  204 us (56%)
  waiting for transfers between devices  126 us (35%)
  between operations  16.2 us (4%)
  matrix products  6.72 us (2%)
  other arithmetic  6.38 us (2%)
    psum x1, waiting for transfers between devices, shards(): whole = lax.psum(partial_all, 'ops')  126 us
    psum x1, blocking collectives, shards(): correlations = lax.psum(local_over, ('ops', 'sec'))  105 us
    psum x1, blocking collectives, shards(): total = lax.psum(jnp.sum(resid * resid), ('ops', 'sec'))  99.5 us
  transfers between devices with their start and end apart: 1, of which 1 were waited for; matrix products, arithmetic and copies ran while one was open for 0% of the time, Pallas kernels for 0%

commit v1 on v0

--- a/solution.py
+++ b/solution.py
@@ -2,6 +2,21 @@
 import jax.numpy as jnp
 from jax import lax
 from jax.sharding import PartitionSpec as P
+
+
+def reduce_rows(partial, shard_rows):
+    n = lax.axis_size("ops")
+    blocks = partial.reshape(n, shard_rows, partial.shape[2])
+    got = lax.all_to_all(blocks, "ops", 0, 0, tiled=True)
+    return jnp.sum(got, axis=0, keepdims=True)
+
+
+def small_sum(v):
+    for ax in ("ops", "sec"):
+        n = lax.axis_size(ax)
+        x = jnp.broadcast_to(v.reshape(1, -1), (n, v.size))
+        v = jnp.sum(lax.all_to_all(x, ax, 0, 0, tiled=True), axis=0).reshape(v.shape)
+    return v
 
 
 def shards(wave, left_ops, right_ops, priors, row_sizes, col_sizes):
@@ -18,17 +33,16 @@
         "sab,ksjb->ksaj", masked, right_ops, preferred_element_type=jnp.float32
     ).astype(jnp.bfloat16)
     partial_all = jnp.einsum("ksia,ksaj->sij", left_ops, inner, preferred_element_type=jnp.float32)
-    whole = lax.psum(partial_all, "ops")
-    summed = lax.dynamic_slice_in_dim(whole, first_row, shard_rows, 1)
+    summed = reduce_rows(partial_all, shard_rows)
     mine_rows = lax.dynamic_slice_in_dim(row_mask, first_row, shard_rows, 1)
     mine_mask = mine_rows[:, :, None] * col_mask[:, None, :]
     sigma = (summed * mine_mask).astype(jnp.bfloat16)
     pmask = (priors * mine_mask[None].astype(jnp.bfloat16)).astype(jnp.float32)
     sig32 = sigma.astype(jnp.float32)
     local_over = jnp.einsum("psab,sab->p", pmask, sig32, precision=lax.Precision.HIGHEST)
-    correlations = lax.psum(local_over, ("ops", "sec"))
+    correlations = small_sum(local_over)
     resid = sig32 - jnp.einsum("p,psab->sab", correlations, pmask, precision=lax.Precision.HIGHEST)
-    total = lax.psum(jnp.sum(resid * resid), ("ops", "sec"))
+    total = small_sum(jnp.sum(resid * resid))
     cells = sec_local * lax.axis_size("sec") * width * width
     new_dir = (resid / jnp.sqrt(total / cells + 1e-06)).astype(jnp.bfloat16)
     return (sigma, new_dir, correlations)

time: 363 us -> 125 us (0.34)
  blocking collectives: 204 us -> 53.6 us
  waiting for transfers between devices: 126 us -> 37 us
  between operations: 16.2 us -> 2.82 us
  starting transfers between devices: 0.04 us -> 13.4 us
    psum x2 -> x0, blocking collectives: 204 us -> none  [the longest x1 105 us: shards(): correlations = lax.psum(local_over, ('ops', 'sec'))]
    psum x1 -> x0, waiting for transfers between devices: 126 us -> none  [shards(): whole = lax.psum(partial_all, 'ops')]
    all_to_all x0 -> x3, blocking collectives: none -> 53.6 us  [small_sum(): lax.all_to_all(x, ax, 0, 0, tiled=True)]
    all_to_all x0 -> x2, waiting for transfers between devices: none -> 37 us  [the longest x1 25.9 us: reduce_rows(): got = lax.all_to_all(blocks, 'ops', 0, 0, tiled=True)]
    all_to_all x0 -> x2, starting transfers between devices: none -> 13.4 us  [the longest x1 7.57 us: reduce_rows(): got = lax.all_to_all(blocks, 'ops', 0, 0, tiled=True)]
  transfers between devices with their start and end apart: 1 -> 2, of which waited for: 1 -> 2; matrix products, arithmetic and copies ran while one was open for 0% -> 2% of each run, Pallas kernels for 0% -> 0%
where the time goes in v1:
time: 125 us
  blocking collectives  53.6 us (43%)
  waiting for transfers between devices  37 us (30%)
  starting transfers between devices  13.4 us (11%)
  matrix products  8.68 us (7%)
  other arithmetic  7.35 us (6%)
  between operations  2.82 us (2%)
  local copies, waits for them, and re-layouts  1.95 us (2%)
    all_to_all x3, blocking collectives, small_sum(): lax.all_to_all(x, ax, 0, 0, tiled=True)  53.6 us
    all_to_all x1, waiting for transfers between devices, reduce_rows(): got = lax.all_to_all(blocks, 'ops', 0, 0, tiled=True)  25.9 us
    all_to_all x1, waiting for transfers between devices, small_sum(): lax.all_to_all(x, ax, 0, 0, tiled=True)  11.1 us
    all_to_all x1, starting transfers between devices, reduce_rows(): got = lax.all_to_all(blocks, 'ops', 0, 0, tiled=True)  7.57 us
    dot_general x1, matrix products, shards(): jnp.einsum('ksia,ksaj->sij', left_ops, inner, preferred_element_type=jnp....  6.46 us
    all_to_all x1, starting transfers between devices, small_sum(): lax.all_to_all(x, ax, 0, 0, tiled=True)  5.82 us
  transfers between devices with their start and end apart: 2, of which 2 were waited for; matrix products, arithmetic and copies ran while one was open for 2% of the time, Pallas kernels for 0%

profile of v1, /device:TPU:1, one launch (start us, length us, event | category | flops | bytes accessed | tf_op | source)
XLA Modules:
  0.0 124.8 jit_solution(18205747612216544251)
XLA Ops:
  0.6 0.0 copy-start
  2.1 6.5 %convolution_bitcast_fusion = f32[16,48,768]{2,1,0:T(8,128)} fusion(bf16[16,48,768]{2,1,0:T(8,128)(2,1)S(1)} %bitcast.63, bf16[1,768,768]{2,1,0:T(8,128)(2,1)} %param.6, bf16[1,1,768,768]{3,2,1,0:T(8,128)(2,1)} %param.8, f32[768]{0:T(1024)S(1)} %get-tuple-element.4, f32[768]{0:T(1024)S(1)} %get-tuple-element.3), kind=kOutput, calls=%fused_computation.1 | convolution fusion | flops 1814298624 | bytes 5904384 | tf_op jit(solution)/shard_map/ksia,ksaj->sij/dot_general | solution.py:35
  8.5 7.6 %all-to-all-start = ((f32[16,48,768]{2,1,0:T(8,128)}), f32[16,48,768]{2,1,0:T(8,128)S(1)}, u32[]{:S(2)}, u32[]{:S(2)}) async-start(f32[16,48,768]{2,1,0:T(8,128)} %convolution_bitcast_fusion), calls=%async_computation | async-start | bytes 4718592 | tf_op jit(solution)/shard_map/all_to_all | solution.py:10
  16.1 0.1 multiply_convert_fusion.1
  16.2 1.9 %multiply_bitcast_fusion = bf16[8,48,768]{2,1,0:T(8,128)(2,1)} fusion(bf16[8,1,48,768]{3,2,1,0:T(8,128)(2,1)} %param.9, bf16[48,768]{1,0:T(8,128)(2,1)S(1)} %multiply_convert_fusion.1), kind=kLoop, calls=%fused_computation.10 | loop fusion | flops 294912 | bytes 1253376 | tf_op jit(solution)/shard_map/reshape.22
  18.1 25.9 %all-to-all-done = f32[16,48,768]{2,1,0:T(8,128)S(1)} async-done(((f32[16,48,768]{2,1,0:T(8,128)}), f32[16,48,768]{2,1,0:T(8,128)S(1)}, u32[]{:S(2)}, u32[]{:S(2)}) %all-to-all-start) | async-done | bytes 2359328 | tf_op jit(solution)/shard_map/all_to_all | solution.py:10
  44.0 0.8 reduce_sum.58
  44.8 1.1 fusion.18
  45.9 1.6 %convolution_bitcast_fusion.1 = f32[8]{0:T(128)S(1)} fusion(bf16[8,48,768]{2,1,0:T(8,128)(2,1)} %multiply_bitcast_fusion, bf16[48,768,1]{1,0,2:T(8,128)(2,1)S(1)} %fusion.18), kind=kOutput, calls=%fused_computation.9 | convolution fusion | flops 589824 | bytes 663584 | tf_op jit(solution)/shard_map/psab,sab->p/dot_general | solution.py:42
  47.5 13.3 %all_to_all.29 = f32[16,1,8]{2,1,0:T(1,128)S(1)} all-to-all(f32[16,1,8]{2,1,0:T(1,128)S(1)} %broadcast_in_dim.8), channel_id=1, replica_groups=mesh['ops'=16,'sec'=32] {'ops'}, dimensions={0} | all-to-all | bytes 1024 | tf_op jit(solution)/shard_map/all_to_all | solution.py:18
  60.8 31.2 %all_to_all.30 = f32[32,1,8]{2,1,0:T(1,128)S(1)} all-to-all(f32[32,1,8]{2,1,0:T(1,128)S(1)} %broadcast_in_dim.9), channel_id=1, replica_groups=mesh['ops'=16,'sec'=32] {'sec'}, dimensions={0} | all-to-all | bytes 2048 | tf_op jit(solution)/shard_map/all_to_all | solution.py:18
  92.0 0.1 reduce_sum.62
  92.0 0.0 copy-start.3
  92.0 0.6 fusion.11
  92.7 0.7 multiply_reduce_fusion
  93.4 0.6 broadcast_in_dim.10
  94.1 9.2 %all_to_all.31 = f32[16,1,1]{2,1,0:T(1,128)S(1)} all-to-all(f32[16,1,1]{2,1,0:T(1,128)S(1)} %broadcast_in_dim.10), channel_id=1, replica_groups=mesh['ops'=16,'sec'=32] {'ops'}, dimensions={0} | all-to-all | bytes 128 | tf_op jit(solution)/shard_map/all_to_all | solution.py:18
  103.2 0.6 reduce_sum.64
  103.8 1.3 %broadcast_in_dim.11 = f32[32,1,1]{2,1,0:T(1,128)} broadcast(f32[]{:T(128)} %reduce_sum.64), dimensions={} | broadcast | bytes 132 | tf_op jit(solution)/shard_map/broadcast_in_dim | solution.py:17
  105.1 5.8 %all-to-all-start.4 = ((f32[32,1,1]{2,1,0:T(1,128)}), f32[32,1,1]{2,1,0:T(1,128)S(1)}, u32[]{:S(2)}, u32[]{:S(2)}) async-start(f32[32,1,1]{2,1,0:T(1,128)} %broadcast_in_dim.11), calls=%async_computation.4 | async-start | bytes 32768 | tf_op jit(solution)/shard_map/all_to_all | solution.py:18
  110.9 0.7 fusion.16
  111.6 11.1 %all-to-all-done.4 = f32[32,1,1]{2,1,0:T(1,128)S(1)} async-done(((f32[32,1,1]{2,1,0:T(1,128)}), f32[32,1,1]{2,1,0:T(1,128)S(1)}, u32[]{:S(2)}, u32[]{:S(2)}) %all-to-all-start.4) | async-done | bytes 160 | tf_op jit(solution)/shard_map/all_to_all | solution.py:18
  122.8 0.6 reduce_sum.65
  124.1 0.7 fusion.19
  (11 shorter events, 0.1 us)
Async XLA Ops:
  0.6 1.4 %copy-start = (bf16[1,1,768,768]{3,2,1,0:T(8,128)(2,1)S(1)}, bf16[1,1,768,768]{3,2,1,0:T(8,128)(2,1)}, u32[]{:S(2)}) copy-start(bf16[1,1,768,768]{3,2,1,0:T(8,128)(2,1)} %param.7) | copy-start | bytes 3538948
  8.5 35.5 %all-to-all-start = ((f32[16,48,768]{2,1,0:T(8,128)}), f32[16,48,768]{2,1,0:T(8,128)S(1)}, u32[]{:S(2)}, u32[]{:S(2)}) async-start(f32[16,48,768]{2,1,0:T(8,128)} %convolution_bitcast_fusion), calls=%async_computation | async-start | bytes 4718592 | tf_op jit(solution)/shard_map/all_to_all | solution.py:10
  44.8 47.2 %copy-start.2 = (bf16[8,48,768]{2,1,0:T(8,128)(2,1)S(1)}, bf16[8,48,768]{2,1,0:T(8,128)(2,1)}, u32[]{:S(2)}) copy-start(bf16[8,48,768]{2,1,0:T(8,128)(2,1)} %multiply_bitcast_fusion) | copy-start | bytes 1769476
  44.8 47.9 %copy-start.1 = (f32[48,768]{1,0:T(8,128)S(1)}, f32[48,768]{1,0:T(8,128)}, u32[]{:S(2)}) copy-start(f32[48,768]{1,0:T(8,128)} %reduce_sum.58) | copy-start | bytes 442372
  92.0 32.8 %copy-start.3 = (f32[8]{0:T(128)}, f32[8]{0:T(128)S(1)}, u32[]{:S(2)}) copy-start(f32[8]{0:T(128)S(1)} %reduce_sum.62) | copy-start | bytes 100
  105.1 17.7 %all-to-all-start.4 = ((f32[32,1,1]{2,1,0:T(1,128)}), f32[32,1,1]{2,1,0:T(1,128)S(1)}, u32[]{:S(2)}, u32[]{:S(2)}) async-start(f32[32,1,1]{2,1,0:T(1,128)} %broadcast_in_dim.11), calls=%async_computation.4 | async-start | bytes 32768 | tf_op jit(solution)/shard_map/all_to_all | solution.py:18

commit v2 on v1

--- a/solution.py
+++ b/solution.py
@@ -40,9 +40,30 @@
     pmask = (priors * mine_mask[None].astype(jnp.bfloat16)).astype(jnp.float32)
     sig32 = sigma.astype(jnp.float32)
     local_over = jnp.einsum("psab,sab->p", pmask, sig32, precision=lax.Precision.HIGHEST)
-    correlations = small_sum(local_over)
+    gram = jnp.einsum("psab,qsab->pq", pmask, pmask, precision=lax.Precision.HIGHEST)
+    sig_sq = jnp.sum(sig32 * sig32)
+    nprior = local_over.shape[0]
+    packed = jnp.concatenate([local_over, gram.reshape(-1), sig_sq[None]])
+    sums = small_sum(packed)
+    correlations = sums[:nprior]
+    gram_all = sums[nprior:-1].reshape(nprior, nprior)
+    sig_sq_all = sums[-1]
     resid = sig32 - jnp.einsum("p,psab->sab", correlations, pmask, precision=lax.Precision.HIGHEST)
-    total = small_sum(jnp.sum(resid * resid))
+    expanded = (
+        sig_sq_all
+        - 2.0 * jnp.dot(correlations, correlations, precision=lax.Precision.HIGHEST)
+        + jnp.dot(
+            correlations,
+            jnp.dot(gram_all, correlations, precision=lax.Precision.HIGHEST),
+            precision=lax.Precision.HIGHEST,
+        )
+    )
+    total = lax.cond(
+        expanded >= sig_sq_all * 0.0625,
+        lambda r: expanded,
+        lambda r: small_sum(jnp.sum(r * r)),
+        resid,
+    )
     cells = sec_local * lax.axis_size("sec") * width * width
     new_dir = (resid / jnp.sqrt(total / cells + 1e-06)).astype(jnp.bfloat16)
     return (sigma, new_dir, correlations)

time: 125 us -> 104 us (0.83)
  blocking collectives: 53.6 us -> 13.3 us
  starting transfers between devices: 13.4 us -> 27.1 us
  between operations: 2.82 us -> 5.5 us
  waiting for transfers between devices: 37 us -> 38.9 us
    all_to_all x3 -> x1, blocking collectives: 53.6 us -> 13.3 us  [small_sum(): lax.all_to_all(x, ax, 0, 0, tiled=True)]
    all_to_all x1, starting transfers between devices: 5.82 us -> 19.5 us  [small_sum(): lax.all_to_all(x, ax, 0, 0, tiled=True)]
    all_to_all x1, waiting for transfers between devices: 25.9 us -> 27.9 us  [reduce_rows(): got = lax.all_to_all(blocks, 'ops', 0, 0, tiled=True)]
    broadcast_in_dim x4 -> x2, local copies, waits for them, and re-layouts: 1.93 us -> 0.63 us  [small_sum(): x = jnp.broadcast_to(v.reshape(1, -1), (n, v.size))]
    reduce_sum x4 -> x2, other arithmetic: 1.34 us -> 0.04 us  [small_sum(): jnp.sum(lax.all_to_all(x, ax, 0, 0, tiled=True), axis=0).reshape(v.shape)]
    dot_general x0 -> x2, matrix products: none -> 1.26 us  [the longest x1 0.74 us: shards(): jnp.dot(gram_all, correlations, precision=lax.Precision.HIGHEST)]
  transfers between devices with their start and end apart: 2 -> 2, of which waited for: 2 -> 2; matrix products, arithmetic and copies ran while one was open for 2% -> 1% of each run, Pallas kernels for 0% -> 0%
where the time goes in v2:
time: 104 us; the launch traced here: 103 us
  waiting for transfers between devices  38.9 us (37%)
  starting transfers between devices  27.1 us (26%)
  blocking collectives  13.3 us (13%)
  matrix products  8.89 us (9%)
  other arithmetic  7.34 us (7%)
  between operations  5.5 us (5%)
  local copies, waits for them, and re-layouts  1.54 us (1%)
    all_to_all x1, waiting for transfers between devices, reduce_rows(): got = lax.all_to_all(blocks, 'ops', 0, 0, tiled=True)  27.9 us
    all_to_all x1, starting transfers between devices, small_sum(): lax.all_to_all(x, ax, 0, 0, tiled=True)  19.5 us
    all_to_all x1, blocking collectives, small_sum(): lax.all_to_all(x, ax, 0, 0, tiled=True)  13.3 us
    all_to_all x1, waiting for transfers between devices, small_sum(): lax.all_to_all(x, ax, 0, 0, tiled=True)  11 us
    all_to_all x1, starting transfers between devices, reduce_rows(): got = lax.all_to_all(blocks, 'ops', 0, 0, tiled=True)  7.57 us
    dot_general x1, matrix products, shards(): jnp.einsum('ksia,ksaj->sij', left_ops, inner, preferred_element_type=jnp....  6.46 us
  transfers between devices with their start and end apart: 2, of which 2 were waited for; matrix products, arithmetic and copies ran while one was open for 1% of the time, Pallas kernels for 0%

profile of v2, /device:TPU:1, one launch (start us, length us, event | category | flops | bytes accessed | tf_op | source)
XLA Modules:
  0.0 103.1 jit_solution(1482995545287894854)
XLA Ops:
  2.1 6.5 %convolution_bitcast_fusion = f32[16,48,768]{2,1,0:T(8,128)} fusion(bf16[16,48,768]{2,1,0:T(8,128)(2,1)S(1)} %bitcast.73, bf16[1,768,768]{2,1,0:T(8,128)(2,1)} %param.8, bf16[1,1,768,768]{3,2,1,0:T(8,128)(2,1)} %param.10, f32[768]{0:T(1024)S(1)} %get-tuple-element.14, f32[768]{0:T(1024)S(1)} %get-tuple-element.13), kind=kOutput, calls=%fused_computation.2 | convolution fusion | flops 1814298624 | bytes 5904384 | tf_op jit(solution)/shard_map/ksia,ksaj->sij/dot_general | solution.py:35
  8.5 7.6 %all-to-all-start.2 = ((f32[16,48,768]{2,1,0:T(8,128)}), f32[16,48,768]{2,1,0:T(8,128)S(1)}, u32[]{:S(2)}, u32[]{:S(2)}) async-start(f32[16,48,768]{2,1,0:T(8,128)} %convolution_bitcast_fusion), calls=%async_computation.2 | async-start | bytes 4718592 | tf_op jit(solution)/shard_map/all_to_all | solution.py:10
  16.1 27.9 %all-to-all-done.2 = f32[16,48,768]{2,1,0:T(8,128)S(1)} async-done(((f32[16,48,768]{2,1,0:T(8,128)}), f32[16,48,768]{2,1,0:T(8,128)S(1)}, u32[]{:S(2)}, u32[]{:S(2)}) %all-to-all-start.2) | async-done | bytes 2359328 | tf_op jit(solution)/shard_map/all_to_all | solution.py:10
  44.0 0.8 reduce_sum.67
  44.8 1.0 fusion.22
  45.8 1.6 %fusion.17 = (f32[]{:T(128)}, bf16[48,768]{1,0:T(8,128)(2,1)S(1)}) fusion(f32[48,768]{1,0:T(8,128)} %reduce_sum.67, f32[768]{0:T(1024)S(1)} %get-tuple-element.14, f32[48]{0:T(128)S(1)} %fusion.26), kind=kLoop, calls=%fused_computation.24 | loop fusion | flops 258047 | bytes 224452 | tf_op jit(solution)/shard_map/reduce_sum | solution.py:44
  47.4 1.1 %multiply_bitcast_fusion = bf16[8,48,768]{2,1,0:T(8,128)(2,1)S(1)} fusion(bf16[8,1,48,768]{3,2,1,0:T(8,128)(2,1)} %param.11, bf16[48,768]{1,0:T(8,128)(2,1)S(1)} %get-tuple-element.12), kind=kLoop, calls=%fused_computation.14 | loop fusion | flops 294912 | bytes 1253376 | tf_op jit(solution)/shard_map/reshape.27
  48.5 0.5 convolution_bitcast_fusion.1
  49.1 0.5 convolution_bitcast_fusion.3
  49.6 0.1 reshape.359
  49.7 0.7 pad_maximum_fusion
  50.4 13.3 %all_to_all.29 = f32[16,1,73]{2,1,0:T(1,128)S(1)} all-to-all(f32[16,1,73]{2,1,0:T(1,128)S(1)} %broadcast_in_dim.11), channel_id=1, replica_groups=mesh['ops'=16,'sec'=32] {'ops'}, dimensions={0} | all-to-all | bytes 9344 | tf_op jit(solution)/shard_map/all_to_all | solution.py:18
  63.7 0.6 broadcast_in_dim.12
  64.3 19.5 %all-to-all-start.4 = ((f32[32,1,73]{2,1,0:T(1,128)}), f32[32,1,73]{2,1,0:T(1,128)S(1)}, u32[]{:S(2)}, u32[]{:S(2)}) async-start(f32[32,1,73]{2,1,0:T(1,128)} %broadcast_in_dim.12), calls=%async_computation.4 | async-start | bytes 32768 | tf_op jit(solution)/shard_map/all_to_all | solution.py:18
  83.9 0.7 fusion.20
  84.6 11.0 %all-to-all-done.4 = f32[32,1,73]{2,1,0:T(1,128)S(1)} async-done(((f32[32,1,73]{2,1,0:T(1,128)}), f32[32,1,73]{2,1,0:T(1,128)S(1)}, u32[]{:S(2)}, u32[]{:S(2)}) %all-to-all-start.4) | async-done | bytes 9376 | tf_op jit(solution)/shard_map/all_to_all | solution.py:18
  95.7 0.7 slice.10
  96.4 0.6 multiply_reduce_fusion.1
  99.0 0.6 fusion.13
  99.7 0.1 convert_subtract_fusion
  99.8 0.1 reshape.360
  99.8 0.7 fusion.12
  101.2 0.5 conditional.1
  102.5 0.6 fusion.23
  (12 shorter events, 0.1 us)
Async XLA Ops:
  0.6 1.4 %copy-start = (bf16[1,1,768,768]{3,2,1,0:T(8,128)(2,1)S(1)}, bf16[1,1,768,768]{3,2,1,0:T(8,128)(2,1)}, u32[]{:S(2)}) copy-start(bf16[1,1,768,768]{3,2,1,0:T(8,128)(2,1)} %param.9) | copy-start | bytes 3538948
  8.5 35.5 %all-to-all-start.2 = ((f32[16,48,768]{2,1,0:T(8,128)}), f32[16,48,768]{2,1,0:T(8,128)S(1)}, u32[]{:S(2)}, u32[]{:S(2)}) async-start(f32[16,48,768]{2,1,0:T(8,128)} %convolution_bitcast_fusion), calls=%async_computation.2 | async-start | bytes 4718592 | tf_op jit(solution)/shard_map/all_to_all | solution.py:10
  48.5 35.4 %copy-start.1 = (f32[48,768]{1,0:T(8,128)S(1)}, f32[48,768]{1,0:T(8,128)}, u32[]{:S(2)}) copy-start(f32[48,768]{1,0:T(8,128)} %reduce_sum.67) | copy-start | bytes 442372
  64.3 31.3 %all-to-all-start.4 = ((f32[32,1,73]{2,1,0:T(1,128)}), f32[32,1,73]{2,1,0:T(1,128)S(1)}, u32[]{:S(2)}, u32[]{:S(2)}) async-start(f32[32,1,73]{2,1,0:T(1,128)} %broadcast_in_dim.12), calls=%async_computation.4 | async-start | bytes 32768 | tf_op jit(solution)/shard_map/all_to_all | solution.py:18
  97.0 6.1 %copy-start.2 = (f32[8]{0:T(128)}, f32[8]{0:T(128)S(1)}, u32[]{:S(2)}) copy-start(f32[8]{0:T(128)S(1)} %get-tuple-element.10) | copy-start | bytes 100

commit v3 on v2

--- a/solution.py
+++ b/solution.py
@@ -12,7 +12,7 @@
 
 
 def small_sum(v):
-    for ax in ("ops", "sec"):
+    for ax in ("sec", "ops"):
         n = lax.axis_size(ax)
         x = jnp.broadcast_to(v.reshape(1, -1), (n, v.size))
         v = jnp.sum(lax.all_to_all(x, ax, 0, 0, tiled=True), axis=0).reshape(v.shape)
@@ -36,11 +36,15 @@
     summed = reduce_rows(partial_all, shard_rows)
     mine_rows = lax.dynamic_slice_in_dim(row_mask, first_row, shard_rows, 1)
     mine_mask = mine_rows[:, :, None] * col_mask[:, None, :]
+    own_rows = first_row + jnp.arange(shard_rows, dtype=jnp.int32)
+    prior_ok = (own_rows[None, :, None] + 1 <= row_sizes[:, None, None]) & (
+        place[None, None, :] + 1 <= col_sizes[:, None, None]
+    )
+    pmask = jnp.where(prior_ok[None], priors, jnp.zeros_like(priors)).astype(jnp.float32)
+    gram = jnp.einsum("psab,qsab->pq", pmask, pmask, precision=lax.Precision.HIGHEST)
     sigma = (summed * mine_mask).astype(jnp.bfloat16)
-    pmask = (priors * mine_mask[None].astype(jnp.bfloat16)).astype(jnp.float32)
     sig32 = sigma.astype(jnp.float32)
     local_over = jnp.einsum("psab,sab->p", pmask, sig32, precision=lax.Precision.HIGHEST)
-    gram = jnp.einsum("psab,qsab->pq", pmask, pmask, precision=lax.Precision.HIGHEST)
     sig_sq = jnp.sum(sig32 * sig32)
     nprior = local_over.shape[0]
     packed = jnp.concatenate([local_over, gram.reshape(-1), sig_sq[None]])

time: 104 us -> 102 us (0.981)
  blocking collectives: 13.3 us -> 33.6 us
  starting transfers between devices: 27.1 us -> 11 us
  waiting for transfers between devices: 38.9 us -> 30.8 us
    all_to_all x1, blocking collectives: 13.3 us -> 33.6 us  [small_sum(): lax.all_to_all(x, ax, 0, 0, tiled=True)]
    all_to_all x1, starting transfers between devices: 19.5 us -> 3.47 us  [small_sum(): lax.all_to_all(x, ax, 0, 0, tiled=True)]
    all_to_all x1, waiting for transfers between devices: 11 us -> 5.57 us  [small_sum(): lax.all_to_all(x, ax, 0, 0, tiled=True)]
    all_to_all x1, waiting for transfers between devices: 27.9 us -> 25.2 us  [reduce_rows(): got = lax.all_to_all(blocks, 'ops', 0, 0, tiled=True)]
    dot_general x1, matrix products: 0.53 us -> 1.58 us  [shards(): jnp.einsum('psab,sab->p', pmask, sig32, precision=lax.Precision.HIGHEST)]
  transfers between devices with their start and end apart: 2 -> 2, of which waited for: 2 -> 2; matrix products, arithmetic and copies ran while one was open for 1% -> 3% of each run, Pallas kernels for 0% -> 0%
where the time goes in v3:
time: 102 us; the launch traced here: 101 us
  blocking collectives  33.6 us (33%)
  waiting for transfers between devices  30.8 us (30%)
  starting transfers between devices  11 us (11%)
  matrix products  9.93 us (10%)
  other arithmetic  7.53 us (7%)
  between operations  5.42 us (5%)
  local copies, waits for them, and re-layouts  2.35 us (2%)
    all_to_all x1, blocking collectives, small_sum(): lax.all_to_all(x, ax, 0, 0, tiled=True)  33.6 us
    all_to_all x1, waiting for transfers between devices, reduce_rows(): got = lax.all_to_all(blocks, 'ops', 0, 0, tiled=True)  25.2 us
    all_to_all x1, starting transfers between devices, reduce_rows(): got = lax.all_to_all(blocks, 'ops', 0, 0, tiled=True)  7.57 us
    dot_general x1, matrix products, shards(): jnp.einsum('ksia,ksaj->sij', left_ops, inner, preferred_element_type=jnp....  6.46 us
    all_to_all x1, waiting for transfers between devices, small_sum(): lax.all_to_all(x, ax, 0, 0, tiled=True)  5.57 us
    all_to_all x1, starting transfers between devices, small_sum(): lax.all_to_all(x, ax, 0, 0, tiled=True)  3.47 us
  transfers between devices with their start and end apart: 2, of which 2 were waited for; matrix products, arithmetic and copies ran while one was open for 3% of the time, Pallas kernels for 0%

profile of v3, /device:TPU:1, one launch (start us, length us, event | category | flops | bytes accessed | tf_op | source)
XLA Modules:
  0.0 101.2 jit_solution(6714422372278318194)
XLA Ops:
  2.1 6.5 %convolution_bitcast_fusion = f32[16,48,768]{2,1,0:T(8,128)} fusion(bf16[16,48,768]{2,1,0:T(8,128)(2,1)S(1)} %bitcast.75, bf16[1,768,768]{2,1,0:T(8,128)(2,1)} %param.8, bf16[1,1,768,768]{3,2,1,0:T(8,128)(2,1)} %param.10, f32[768]{0:T(1024)S(1)} %get-tuple-element.12, f32[768]{0:T(1024)S(1)} %get-tuple-element.11), kind=kOutput, calls=%fused_computation.2 | convolution fusion | flops 1814298624 | bytes 5904384 | tf_op jit(solution)/shard_map/ksia,ksaj->sij/dot_general | solution.py:35
  8.5 7.6 %all-to-all-start.2 = ((f32[16,48,768]{2,1,0:T(8,128)}), f32[16,48,768]{2,1,0:T(8,128)S(1)}, u32[]{:S(2)}, u32[]{:S(2)}) async-start(f32[16,48,768]{2,1,0:T(8,128)} %convolution_bitcast_fusion), calls=%async_computation.2 | async-start | bytes 4718592 | tf_op jit(solution)/shard_map/all_to_all | solution.py:10
  16.1 0.1 broadcast_and_fusion
  16.2 1.1 %select_bitcast_fusion = bf16[8,48,768]{2,1,0:T(8,128)(2,1)S(1)} fusion(bf16[8,1,48,768]{3,2,1,0:T(8,128)(2,1)} %param.11, pred[48,768]{1,0:T(8,128)(4,1)S(1)} %broadcast_and_fusion), kind=kLoop, calls=%fused_computation.14 | loop fusion | flops 294912 | bytes 1216512 | tf_op jit(solution)/shard_map/reshape.31
  17.3 0.8 copy-done.2
  18.2 0.5 convolution_bitcast_fusion.1
  18.8 25.2 %all-to-all-done.2 = f32[16,48,768]{2,1,0:T(8,128)S(1)} async-done(((f32[16,48,768]{2,1,0:T(8,128)}), f32[16,48,768]{2,1,0:T(8,128)S(1)}, u32[]{:S(2)}, u32[]{:S(2)}) %all-to-all-start.2) | async-done | bytes 2359328 | tf_op jit(solution)/shard_map/all_to_all | solution.py:10
  44.0 0.8 reduce_sum.67
  44.8 1.1 %fusion.21 = bf16[48,768,1]{1,0,2:T(8,128)(2,1)S(1)} fusion(f32[48,768]{1,0:T(8,128)} %reduce_sum.67, f32[768]{0:T(1024)S(1)} %get-tuple-element.12, f32[48]{0:T(128)S(1)} %fusion.25), kind=kLoop, calls=%fused_computation.30 | loop fusion | flops 110592 | bytes 224448 | tf_op jit(solution)/shard_map/convert_element_type | solution.py:45
  45.9 1.6 %fusion.17 = f32[]{:T(128)} fusion(f32[48,768]{1,0:T(8,128)} %reduce_sum.67, f32[768]{0:T(1024)S(1)} %get-tuple-element.12, f32[48]{0:T(128)S(1)} %fusion.25), kind=kLoop, calls=%fused_computation.22 | loop fusion | flops 221183 | bytes 150724 | tf_op jit(solution)/shard_map/reduce_sum | solution.py:48
  47.5 1.6 %convolution_bitcast_fusion.3 = f32[8]{0:T(128)S(1)} fusion(bf16[8,48,768]{2,1,0:T(8,128)(2,1)} %copy-done.2, bf16[48,768,1]{1,0,2:T(8,128)(2,1)S(1)} %fusion.21), kind=kOutput, calls=%fused_computation.12 | convolution fusion | flops 589824 | bytes 663584 | tf_op jit(solution)/shard_map/psab,sab->p/dot_general | solution.py:47
  49.1 0.7 pad_maximum_fusion
  49.8 33.6 %all_to_all.29 = f32[32,1,73]{2,1,0:T(1,128)S(1)} all-to-all(f32[32,1,73]{2,1,0:T(1,128)S(1)} %broadcast_in_dim.23), channel_id=1, replica_groups=mesh['ops'=16,'sec'=32] {'sec'}, dimensions={0} | all-to-all | bytes 18688 | tf_op jit(solution)/shard_map/all_to_all | solution.py:18
  83.5 0.6 broadcast_in_dim.24
  84.1 3.5 %all-to-all-start.4 = ((f32[16,1,73]{2,1,0:T(1,128)}), f32[16,1,73]{2,1,0:T(1,128)S(1)}, u32[]{:S(2)}, u32[]{:S(2)}) async-start(f32[16,1,73]{2,1,0:T(1,128)} %broadcast_in_dim.24), calls=%async_computation.4 | async-start | bytes 16384 | tf_op jit(solution)/shard_map/all_to_all | solution.py:18
  87.6 0.7 fusion.19
  88.3 5.6 %all-to-all-done.4 = f32[16,1,73]{2,1,0:T(1,128)S(1)} async-done(((f32[16,1,73]{2,1,0:T(1,128)}), f32[16,1,73]{2,1,0:T(1,128)S(1)}, u32[]{:S(2)}, u32[]{:S(2)}) %all-to-all-start.4) | async-done | bytes 4704 | tf_op jit(solution)/shard_map/all_to_all | solution.py:18
  94.0 0.6 multiply_reduce_fusion.1
  94.6 0.7 slice.10
  95.3 0.6 fusion.13
  96.0 0.7 fusion.12
  99.3 0.1 convert_subtract_fusion
  99.4 0.5 conditional.1
  100.6 0.6 fusion.22
  (19 shorter events, 0.3 us)
Async XLA Ops:
  0.6 1.4 %copy-start = (bf16[1,1,768,768]{3,2,1,0:T(8,128)(2,1)S(1)}, bf16[1,1,768,768]{3,2,1,0:T(8,128)(2,1)}, u32[]{:S(2)}) copy-start(bf16[1,1,768,768]{3,2,1,0:T(8,128)(2,1)} %param.9) | copy-start | bytes 3538948
  8.5 35.5 %all-to-all-start.2 = ((f32[16,48,768]{2,1,0:T(8,128)}), f32[16,48,768]{2,1,0:T(8,128)S(1)}, u32[]{:S(2)}, u32[]{:S(2)}) async-start(f32[16,48,768]{2,1,0:T(8,128)} %convolution_bitcast_fusion), calls=%async_computation.2 | async-start | bytes 4718592 | tf_op jit(solution)/shard_map/all_to_all | solution.py:10
  17.3 0.8 copy-start.2
  44.8 42.8 %copy-start.1 = (f32[48,768]{1,0:T(8,128)S(1)}, f32[48,768]{1,0:T(8,128)}, u32[]{:S(2)}) copy-start(f32[48,768]{1,0:T(8,128)} %reduce_sum.67) | copy-start | bytes 442372
  44.8 50.5 %copy-start.3 = (bf16[8,48,768]{2,1,0:T(8,128)(2,1)S(1)}, bf16[8,48,768]{2,1,0:T(8,128)(2,1)}, u32[]{:S(2)}) copy-start(bf16[8,48,768]{2,1,0:T(8,128)(2,1)} %copy-done.2) | copy-start | bytes 1769476
  84.1 9.8 %all-to-all-start.4 = ((f32[16,1,73]{2,1,0:T(1,128)}), f32[16,1,73]{2,1,0:T(1,128)S(1)}, u32[]{:S(2)}, u32[]{:S(2)}) async-start(f32[16,1,73]{2,1,0:T(1,128)} %broadcast_in_dim.24), calls=%async_computation.4 | async-start | bytes 16384 | tf_op jit(solution)/shard_map/all_to_all | solution.py:18
  94.6 6.7 %copy-start.4 = (f32[8]{0:T(128)}, f32[8]{0:T(128)S(1)}, u32[]{:S(2)}) copy-start(f32[8]{0:T(128)S(1)} %get-tuple-element.10) | copy-start | bytes 100

commit v4 on v3

--- a/solution.py
+++ b/solution.py
@@ -44,7 +44,7 @@
     gram = jnp.einsum("psab,qsab->pq", pmask, pmask, precision=lax.Precision.HIGHEST)
     sigma = (summed * mine_mask).astype(jnp.bfloat16)
     sig32 = sigma.astype(jnp.float32)
-    local_over = jnp.einsum("psab,sab->p", pmask, sig32, precision=lax.Precision.HIGHEST)
+    local_over = jnp.sum(pmask * sig32[None], axis=(1, 2, 3))
     sig_sq = jnp.sum(sig32 * sig32)
     nprior = local_over.shape[0]
     packed = jnp.concatenate([local_over, gram.reshape(-1), sig_sq[None]])
@@ -52,7 +52,7 @@
     correlations = sums[:nprior]
     gram_all = sums[nprior:-1].reshape(nprior, nprior)
     sig_sq_all = sums[-1]
-    resid = sig32 - jnp.einsum("p,psab->sab", correlations, pmask, precision=lax.Precision.HIGHEST)
+    resid = sig32 - jnp.sum(correlations[:, None, None, None] * pmask, axis=0)
     expanded = (
         sig_sq_all
         - 2.0 * jnp.dot(correlations, correlations, precision=lax.Precision.HIGHEST)

time: 102 us -> 99.7 us (0.977)
  blocking collectives: 33.6 us -> 43 us
  waiting for transfers between devices: 30.8 us -> 25.4 us
  starting transfers between devices: 11 us -> 7.57 us
  matrix products: 9.93 us -> 7.72 us
    all_to_all x1 -> x2, blocking collectives: 33.6 us -> 43 us  [small_sum(): lax.all_to_all(x, ax, 0, 0, tiled=True)]
    all_to_all x1 -> x0, waiting for transfers between devices: 5.57 us -> none  [small_sum(): lax.all_to_all(x, ax, 0, 0, tiled=True)]
    all_to_all x1 -> x0, starting transfers between devices: 3.47 us -> none  [small_sum(): lax.all_to_all(x, ax, 0, 0, tiled=True)]
    dot_general x2 -> x0, matrix products: 2.22 us -> none  [the longest x1 1.58 us: shards(): jnp.einsum('psab,sab->p', pmask, sig32, precision=lax.Precision.HIGHEST)]
    convert_element_type x2 -> x0, other arithmetic: 1.78 us -> none  [shards(): sigma = (summed * mine_mask).astype(jnp.bfloat16)]
    reduce_sum x0 -> x2, other arithmetic: none -> 1.54 us  [the longest x1 1.37 us: shards(): local_over = jnp.sum(pmask * sig32[None], axis=(1, 2, 3))]
  transfers between devices with their start and end apart: 2 -> 1, of which waited for: 2 -> 1; matrix products, arithmetic and copies ran while one was open for 3% -> 2% of each run, Pallas kernels for 0% -> 0%
where the time goes in v4:
time: 99.7 us; the launch traced here: 99.3 us
  blocking collectives  43 us (43%)
  waiting for transfers between devices  25.4 us (25%)
  other arithmetic  8.04 us (8%)
  matrix products  7.72 us (8%)
  starting transfers between devices  7.57 us (8%)
  between operations  5.4 us (5%)
  local copies, waits for them, and re-layouts  1.52 us (2%)
    all_to_all x2, blocking collectives, small_sum(): lax.all_to_all(x, ax, 0, 0, tiled=True)  43 us
    all_to_all x1, waiting for transfers between devices, reduce_rows(): got = lax.all_to_all(blocks, 'ops', 0, 0, tiled=True)  25.4 us
    all_to_all x1, starting transfers between devices, reduce_rows(): got = lax.all_to_all(blocks, 'ops', 0, 0, tiled=True)  7.57 us
    dot_general x1, matrix products, shards(): jnp.einsum('ksia,ksaj->sij', left_ops, inner, preferred_element_type=jnp....  6.46 us
  transfers between devices with their start and end apart: 1, of which 1 were waited for; matrix products, arithmetic and copies ran while one was open for 2% of the time, Pallas kernels for 0%

profile of v4, /device:TPU:1, one launch (start us, length us, event | category | flops | bytes accessed | tf_op | source)
XLA Modules:
  0.0 99.3 jit_solution(12658075195042887761)
XLA Ops:
  0.6 0.0 copy-start
  2.1 6.5 %convolution_bitcast_fusion = f32[16,48,768]{2,1,0:T(8,128)} fusion(bf16[16,48,768]{2,1,0:T(8,128)(2,1)S(1)} %bitcast.59, bf16[1,768,768]{2,1,0:T(8,128)(2,1)} %param.8, bf16[1,1,768,768]{3,2,1,0:T(8,128)(2,1)} %param.10, f32[768]{0:T(1024)S(1)} %get-tuple-element.15, f32[768]{0:T(1024)S(1)} %get-tuple-element.14), kind=kOutput, calls=%fused_computation.2 | convolution fusion | flops 1814298624 | bytes 5904384 | tf_op jit(solution)/shard_map/ksia,ksaj->sij/dot_general | solution.py:35
  8.5 7.6 %all-to-all-start.2 = ((f32[16,48,768]{2,1,0:T(8,128)}), f32[16,48,768]{2,1,0:T(8,128)S(1)}, u32[]{:S(2)}, u32[]{:S(2)}) async-start(f32[16,48,768]{2,1,0:T(8,128)} %convolution_bitcast_fusion), calls=%async_computation.2 | async-start | bytes 4718592 | tf_op jit(solution)/shard_map/all_to_all | solution.py:10
  16.1 0.1 broadcast_and_fusion
  16.2 0.6 copy-done.3
  16.8 1.1 %fusion.16 = bf16[8,48,768]{2,1,0:T(8,128)(2,1)S(1)} fusion(bf16[8,1,48,768]{3,2,1,0:T(8,128)(2,1)} %param.11, pred[48,768]{1,0:T(8,128)(4,1)S(1)} %broadcast_and_fusion), kind=kLoop, calls=%fused_computation.20 | loop fusion | flops 294912 | bytes 1216512 | tf_op jit(solution)/shard_map/reshape.32
  17.9 0.5 convolution_bitcast_fusion.1
  18.5 0.1 reshape.465
  18.6 25.4 %all-to-all-done.2 = f32[16,48,768]{2,1,0:T(8,128)S(1)} async-done(((f32[16,48,768]{2,1,0:T(8,128)}), f32[16,48,768]{2,1,0:T(8,128)S(1)}, u32[]{:S(2)}, u32[]{:S(2)}) %all-to-all-start.2) | async-done | bytes 2359328 | tf_op jit(solution)/shard_map/all_to_all | solution.py:10
  44.0 0.8 reduce_sum.85
  44.8 1.7 %multiply_reduce_fusion.1 = (f32[]{:T(128)}, f32[48,768]{1,0:T(8,128)S(1)}) fusion(f32[48,768]{1,0:T(8,128)} %reduce_sum.85, f32[768]{0:T(1024)S(1)} %get-tuple-element.15, f32[48]{0:T(128)S(1)} %fusion.21), kind=kLoop, calls=%fused_computation.25 | loop fusion | flops 221183 | bytes 298180 | tf_op jit(solution)/shard_map/reduce_sum | solution.py:48
  46.5 1.4 %fusion.1 = f32[8]{0:T(128)S(1)} fusion(f32[48,768]{1,0:T(8,128)S(1)} %get-tuple-element.13, bf16[8,1,48,768]{3,2,1,0:T(8,128)(2,1)} %param.11, pred[48,768]{1,0:T(8,128)(4,1)} %copy-done.3), kind=kLoop, calls=%fused_computation.7 | loop fusion | flops 1179640 | bytes 774176 | tf_op jit(solution)/shard_map/reduce_sum | solution.py:47
  47.9 0.7 pad_maximum_fusion
  48.6 33.6 %all_to_all.29 = f32[32,1,73]{2,1,0:T(1,128)S(1)} all-to-all(f32[32,1,73]{2,1,0:T(1,128)S(1)} %broadcast_in_dim.23), channel_id=1, replica_groups=mesh['ops'=16,'sec'=32] {'sec'}, dimensions={0} | all-to-all | bytes 18688 | tf_op jit(solution)/shard_map/all_to_all | solution.py:18
  82.3 9.4 %all_to_all.30 = f32[16,1,73]{2,1,0:T(1,128)S(1)} all-to-all(f32[16,1,73]{2,1,0:T(1,128)S(1)} %broadcast_in_dim.24), channel_id=1, replica_groups=mesh['ops'=16,'sec'=32] {'ops'}, dimensions={0} | all-to-all | bytes 9344 | tf_op jit(solution)/shard_map/all_to_all | solution.py:18
  91.7 0.7 multiply_reduce_fusion.2
  92.4 0.6 slice.10
  93.0 0.1 slice.11
  93.1 0.2 fusion.2
  93.2 0.7 bitcast_subtract_fusion
  94.0 0.1 reshape.466
  94.0 0.7 fusion.15
  97.4 0.5 conditional.1
  98.6 0.6 divide_convert_fusion
  (18 shorter events, 0.1 us)
Async XLA Ops:
  0.6 1.4 %copy-start = (bf16[1,1,768,768]{3,2,1,0:T(8,128)(2,1)S(1)}, bf16[1,1,768,768]{3,2,1,0:T(8,128)(2,1)}, u32[]{:S(2)}) copy-start(bf16[1,1,768,768]{3,2,1,0:T(8,128)(2,1)} %param.9) | copy-start | bytes 3538948
  8.5 35.5 %all-to-all-start.2 = ((f32[16,48,768]{2,1,0:T(8,128)}), f32[16,48,768]{2,1,0:T(8,128)S(1)}, u32[]{:S(2)}, u32[]{:S(2)}) async-start(f32[16,48,768]{2,1,0:T(8,128)} %convolution_bitcast_fusion), calls=%async_computation.2 | async-start | bytes 4718592 | tf_op jit(solution)/shard_map/all_to_all | solution.py:10
  16.2 0.6 copy-start.3
  44.8 48.3 %copy-start.1 = (bf16[8,1,48,768]{3,2,1,0:T(8,128)(2,1)S(1)}, bf16[8,1,48,768]{3,2,1,0:T(8,128)(2,1)}, u32[]{:S(2)}) copy-start(bf16[8,1,48,768]{3,2,1,0:T(8,128)(2,1)} %param.11) | copy-start | bytes 1769476
  44.8 48.3 %copy-start.4 = (pred[48,768]{1,0:T(8,128)(4,1)S(1)}, pred[48,768]{1,0:T(8,128)(4,1)}, u32[]{:S(2)}) copy-start(pred[48,768]{1,0:T(8,128)(4,1)} %copy-done.3) | copy-start | bytes 110596
  44.8 48.4 %copy-start.2 = (f32[48,768]{1,0:T(8,128)S(1)}, f32[48,768]{1,0:T(8,128)}, u32[]{:S(2)}) copy-start(f32[48,768]{1,0:T(8,128)} %reduce_sum.85) | copy-start | bytes 442372
  92.4 6.9 %copy-start.5 = (f32[8]{0:T(128)}, f32[8]{0:T(128)S(1)}, u32[]{:S(2)}) copy-start(f32[8]{0:T(128)S(1)} %get-tuple-element.9) | copy-start | bytes 100

commit v5 on v4

--- a/solution.py
+++ b/solution.py
@@ -53,23 +53,20 @@
     gram_all = sums[nprior:-1].reshape(nprior, nprior)
     sig_sq_all = sums[-1]
     resid = sig32 - jnp.sum(correlations[:, None, None, None] * pmask, axis=0)
-    expanded = (
-        sig_sq_all
-        - 2.0 * jnp.dot(correlations, correlations, precision=lax.Precision.HIGHEST)
-        + jnp.dot(
-            correlations,
-            jnp.dot(gram_all, correlations, precision=lax.Precision.HIGHEST),
-            precision=lax.Precision.HIGHEST,
-        )
-    )
-    total = lax.cond(
+    eye = jnp.eye(nprior, dtype=jnp.float32)
+    expanded = sig_sq_all + jnp.sum(correlations[:, None] * correlations[None, :] * (gram_all - 2.0 * eye))
+    cells = sec_local * lax.axis_size("sec") * width * width
+
+    def scaled(total):
+        return (resid / jnp.sqrt(total / cells + 1e-06)).astype(jnp.bfloat16)
+
+    fast = scaled(expanded)
+    new_dir = lax.cond(
         expanded >= sig_sq_all * 0.0625,
-        lambda r: expanded,
-        lambda r: small_sum(jnp.sum(r * r)),
+        lambda r: fast,
+        lambda r: scaled(small_sum(jnp.sum(r * r))),
         resid,
     )
-    cells = sec_local * lax.axis_size("sec") * width * width
-    new_dir = (resid / jnp.sqrt(total / cells + 1e-06)).astype(jnp.bfloat16)
     return (sigma, new_dir, correlations)
 
 

time: 99.7 us -> 97 us (0.973)
  between operations: 5.4 us -> 4.12 us
where the time goes in v5:
time: 97 us; the launch traced here: 96.6 us
  blocking collectives  43 us (44%)
  waiting for transfers between devices  25.4 us (26%)
  starting transfers between devices  7.57 us (8%)
  other arithmetic  7.4 us (8%)
  matrix products  6.98 us (7%)
  between operations  4.12 us (4%)
  local copies, waits for them, and re-layouts  2.1 us (2%)
    all_to_all x2, blocking collectives, small_sum(): lax.all_to_all(x, ax, 0, 0, tiled=True)  43 us
    all_to_all x1, waiting for transfers between devices, reduce_rows(): got = lax.all_to_all(blocks, 'ops', 0, 0, tiled=True)  25.4 us
    all_to_all x1, starting transfers between devices, reduce_rows(): got = lax.all_to_all(blocks, 'ops', 0, 0, tiled=True)  7.57 us
    dot_general x1, matrix products, shards(): jnp.einsum('ksia,ksaj->sij', left_ops, inner, preferred_element_type=jnp....  6.46 us
  transfers between devices with their start and end apart: 1, of which 1 were waited for; matrix products, arithmetic and copies ran while one was open for 2% of the time, Pallas kernels for 0%

profile of v5, /device:TPU:1, one launch (start us, length us, event | category | flops | bytes accessed | tf_op | source)
XLA Modules:
  0.0 96.6 jit_solution(4927635444100078003)
XLA Ops:
  0.6 0.0 copy-start
  2.0 0.0 copy-done
  2.1 6.5 %convolution_bitcast_fusion = f32[16,48,768]{2,1,0:T(8,128)} fusion(bf16[16,48,768]{2,1,0:T(8,128)(2,1)S(1)} %bitcast.51, bf16[1,768,768]{2,1,0:T(8,128)(2,1)} %param.8, bf16[1,1,768,768]{3,2,1,0:T(8,128)(2,1)} %param.10, f32[768]{0:T(1024)S(1)} %get-tuple-element.14, f32[768]{0:T(1024)S(1)} %get-tuple-element.13), kind=kOutput, calls=%fused_computation.3 | convolution fusion | flops 1814298624 | bytes 5904384 | tf_op jit(solution)/shard_map/ksia,ksaj->sij/dot_general | solution.py:35
  8.5 7.6 %all-to-all-start.2 = ((f32[16,48,768]{2,1,0:T(8,128)}), f32[16,48,768]{2,1,0:T(8,128)S(1)}, u32[]{:S(2)}, u32[]{:S(2)}) async-start(f32[16,48,768]{2,1,0:T(8,128)} %convolution_bitcast_fusion), calls=%async_computation.2 | async-start | bytes 4718592 | tf_op jit(solution)/shard_map/all_to_all | solution.py:10
  16.1 0.1 broadcast_and_fusion
  16.2 0.0 copy-start.3
  16.2 0.6 copy-done.3
  16.8 1.1 %fusion.14 = bf16[8,48,768]{2,1,0:T(8,128)(2,1)S(1)} fusion(bf16[8,1,48,768]{3,2,1,0:T(8,128)(2,1)} %param.11, pred[48,768]{1,0:T(8,128)(4,1)S(1)} %broadcast_and_fusion), kind=kLoop, calls=%fused_computation.18 | loop fusion | flops 294912 | bytes 1216512 | tf_op jit(solution)/shard_map/reshape.32
  17.9 0.5 convolution_bitcast_fusion.1
  18.5 0.1 reshape.475
  18.6 25.4 %all-to-all-done.2 = f32[16,48,768]{2,1,0:T(8,128)S(1)} async-done(((f32[16,48,768]{2,1,0:T(8,128)}), f32[16,48,768]{2,1,0:T(8,128)S(1)}, u32[]{:S(2)}, u32[]{:S(2)}) %all-to-all-start.2) | async-done | bytes 2359328 | tf_op jit(solution)/shard_map/all_to_all | solution.py:10
  44.0 0.8 reduce_sum.94
  44.8 1.7 %multiply_reduce_fusion.1 = (f32[]{:T(128)}, f32[48,768]{1,0:T(8,128)S(1)}) fusion(f32[48,768]{1,0:T(8,128)} %reduce_sum.94, f32[768]{0:T(1024)S(1)} %get-tuple-element.14, f32[48]{0:T(128)S(1)} %fusion.19), kind=kLoop, calls=%fused_computation.23 | loop fusion | flops 221183 | bytes 298180 | tf_op jit(solution)/shard_map/reduce_sum | solution.py:48
  46.5 1.4 %fusion.1 = f32[8]{0:T(128)S(1)} fusion(f32[48,768]{1,0:T(8,128)S(1)} %get-tuple-element.12, bf16[8,1,48,768]{3,2,1,0:T(8,128)(2,1)} %param.11, pred[48,768]{1,0:T(8,128)(4,1)} %copy-done.3), kind=kLoop, calls=%fused_computation.8 | loop fusion | flops 1179640 | bytes 774176 | tf_op jit(solution)/shard_map/reduce_sum | solution.py:47
  47.9 0.7 pad_maximum_fusion
  48.6 33.6 %all_to_all.29 = f32[32,1,73]{2,1,0:T(1,128)S(1)} all-to-all(f32[32,1,73]{2,1,0:T(1,128)S(1)} %broadcast_in_dim.23), channel_id=1, replica_groups=mesh['ops'=16,'sec'=32] {'sec'}, dimensions={0} | all-to-all | bytes 18688 | tf_op jit(solution)/shard_map/all_to_all | solution.py:18
  82.3 9.4 %all_to_all.30 = f32[16,1,73]{2,1,0:T(1,128)S(1)} all-to-all(f32[16,1,73]{2,1,0:T(1,128)S(1)} %broadcast_in_dim.24), channel_id=1, replica_groups=mesh['ops'=16,'sec'=32] {'ops'}, dimensions={0} | all-to-all | bytes 9344 | tf_op jit(solution)/shard_map/all_to_all | solution.py:18
  91.7 0.6 slice.11
  92.3 0.1 slice.13
  92.3 0.1 slice.14
  92.4 0.2 fusion.2
  92.6 0.7 multiply_reduce_fusion.2
  95.3 0.7 divide_convert_fusion.1
  96.0 0.6 copy-done.5
  (18 shorter events, 0.1 us)
Async XLA Ops:
  0.6 1.4 %copy-start = (bf16[1,1,768,768]{3,2,1,0:T(8,128)(2,1)S(1)}, bf16[1,1,768,768]{3,2,1,0:T(8,128)(2,1)}, u32[]{:S(2)}) copy-start(bf16[1,1,768,768]{3,2,1,0:T(8,128)(2,1)} %param.9) | copy-start | bytes 3538948
  8.5 35.5 %all-to-all-start.2 = ((f32[16,48,768]{2,1,0:T(8,128)}), f32[16,48,768]{2,1,0:T(8,128)S(1)}, u32[]{:S(2)}, u32[]{:S(2)}) async-start(f32[16,48,768]{2,1,0:T(8,128)} %convolution_bitcast_fusion), calls=%async_computation.2 | async-start | bytes 4718592 | tf_op jit(solution)/shard_map/all_to_all | solution.py:10
  16.2 0.6 copy-start.3
  44.8 47.6 %copy-start.1 = (bf16[8,1,48,768]{3,2,1,0:T(8,128)(2,1)S(1)}, bf16[8,1,48,768]{3,2,1,0:T(8,128)(2,1)}, u32[]{:S(2)}) copy-start(bf16[8,1,48,768]{3,2,1,0:T(8,128)(2,1)} %param.11) | copy-start | bytes 1769476
  44.8 47.6 %copy-start.4 = (pred[48,768]{1,0:T(8,128)(4,1)S(1)}, pred[48,768]{1,0:T(8,128)(4,1)}, u32[]{:S(2)}) copy-start(pred[48,768]{1,0:T(8,128)(4,1)} %copy-done.3) | copy-start | bytes 110596
  44.8 50.5 %copy-start.2 = (f32[48,768]{1,0:T(8,128)S(1)}, f32[48,768]{1,0:T(8,128)}, u32[]{:S(2)}) copy-start(f32[48,768]{1,0:T(8,128)} %reduce_sum.94) | copy-start | bytes 442372
  91.7 4.3 %copy-start.6 = (f32[73]{0:T(128)}, f32[73]{0:T(128)S(1)}, u32[]{:S(2)}) copy-start(f32[73]{0:T(128)S(1)} %reduce_sum.99) | copy-start | bytes 880
  96.0 0.6 copy-start.5

commit v6 on v5

--- a/solution.py
+++ b/solution.py
@@ -29,10 +29,10 @@
     col_mask = (place[None, :] < col_sizes[:, None]).astype(jnp.float32)
     full_mask = row_mask[:, :, None] * col_mask[:, None, :]
     masked = wave * full_mask.astype(jnp.bfloat16)
-    inner = jnp.einsum(
-        "sab,ksjb->ksaj", masked, right_ops, preferred_element_type=jnp.float32
+    inner = lax.dot_general(
+        masked[0], right_ops[0, 0], (((1,), (1,)), ((), ())), preferred_element_type=jnp.float32
     ).astype(jnp.bfloat16)
-    partial_all = jnp.einsum("ksia,ksaj->sij", left_ops, inner, preferred_element_type=jnp.float32)
+    partial_all = jnp.dot(left_ops[0, 0], inner, preferred_element_type=jnp.float32)[None]
     summed = reduce_rows(partial_all, shard_rows)
     mine_rows = lax.dynamic_slice_in_dim(row_mask, first_row, shard_rows, 1)
     mine_mask = mine_rows[:, :, None] * col_mask[:, None, :]

time: 97 us -> 95.7 us (0.987)
  matrix products: 6.98 us -> 5.61 us
    dot_general x1, matrix products: 6.46 us -> 5.09 us  [shards(): jnp.dot(left_ops[0, 0], inner, preferred_element_type=jnp.float32)[None]]
where the time goes in v6:
time: 95.7 us; the launch traced here: 95.2 us
  blocking collectives  43 us (45%)
  waiting for transfers between devices  25.5 us (27%)
  starting transfers between devices  7.58 us (8%)
  other arithmetic  7.4 us (8%)
  matrix products  5.61 us (6%)
  between operations  4.12 us (4%)
  local copies, waits for them, and re-layouts  2.1 us (2%)
    all_to_all x2, blocking collectives, small_sum(): lax.all_to_all(x, ax, 0, 0, tiled=True)  43 us
    all_to_all x1, waiting for transfers between devices, reduce_rows(): got = lax.all_to_all(blocks, 'ops', 0, 0, tiled=True)  25.5 us
    all_to_all x1, starting transfers between devices, reduce_rows(): got = lax.all_to_all(blocks, 'ops', 0, 0, tiled=True)  7.58 us
    dot_general x1, matrix products, shards(): jnp.dot(left_ops[0, 0], inner, preferred_element_type=jnp.float32)[None]  5.09 us
  transfers between devices with their start and end apart: 1, of which 1 were waited for; matrix products, arithmetic and copies ran while one was open for 2% of the time, Pallas kernels for 0%

profile of v6, /device:TPU:1, one launch (start us, length us, event | category | flops | bytes accessed | tf_op | source)
XLA Modules:
  0.0 95.2 jit_solution(4192499052752712369)
XLA Ops:
  0.6 0.0 copy-start
  2.0 0.0 copy-done
  2.1 5.1 %fusion.5 = f32[768,768]{0,1:T(8,128)} fusion(bf16[1,1,768,768]{3,2,1,0:T(8,128)(2,1)S(1)} %copy-done, bf16[1,768,768]{2,1,0:T(8,128)(2,1)} %param.8, bf16[1,1,768,768]{3,2,1,0:T(8,128)(2,1)} %param.10, f32[768]{0:T(1024)S(1)} %get-tuple-element.14, f32[768]{0:T(1024)S(1)} %get-tuple-element.13), kind=kOutput, calls=%fused_computation.10 | convolution fusion | flops 1814298624 | bytes 5904384 | tf_op jit(solution)/shard_map/dot_general | solution.py:35
  7.1 7.6 %all-to-all-start.2 = ((f32[16,48,768]{2,1,0:T(8,128)}), f32[16,48,768]{2,1,0:T(8,128)S(1)}, u32[]{:S(2)}, u32[]{:S(2)}) async-start(f32[16,48,768]{2,1,0:T(8,128)} %bitcast.42), calls=%async_computation.2 | async-start | bytes 4718592 | tf_op jit(solution)/shard_map/all_to_all | solution.py:10
  14.8 0.1 broadcast_and_fusion
  14.9 0.0 copy-start.3
  14.9 0.6 copy-done.3
  15.5 1.1 %fusion.15 = bf16[8,48,768]{2,1,0:T(8,128)(2,1)S(1)} fusion(bf16[8,1,48,768]{3,2,1,0:T(8,128)(2,1)} %param.11, pred[48,768]{1,0:T(8,128)(4,1)S(1)} %broadcast_and_fusion), kind=kLoop, calls=%fused_computation.18 | loop fusion | flops 294912 | bytes 1216512 | tf_op jit(solution)/shard_map/reshape.24
  16.6 0.5 convolution_bitcast_fusion
  17.1 0.1 reshape.455
  17.2 25.5 %all-to-all-done.2 = f32[16,48,768]{2,1,0:T(8,128)S(1)} async-done(((f32[16,48,768]{2,1,0:T(8,128)}), f32[16,48,768]{2,1,0:T(8,128)S(1)}, u32[]{:S(2)}, u32[]{:S(2)}) %all-to-all-start.2) | async-done | bytes 2359328 | tf_op jit(solution)/shard_map/all_to_all | solution.py:10
  42.7 0.8 reduce_sum.94
  43.5 1.7 %multiply_reduce_fusion.1 = (f32[]{:T(128)}, f32[48,768]{1,0:T(8,128)S(1)}) fusion(f32[48,768]{1,0:T(8,128)} %reduce_sum.94, f32[768]{0:T(1024)S(1)} %get-tuple-element.14, f32[48]{0:T(128)S(1)} %fusion.20), kind=kLoop, calls=%fused_computation.23 | loop fusion | flops 221183 | bytes 298180 | tf_op jit(solution)/shard_map/reduce_sum | solution.py:48
  45.1 1.4 %fusion = f32[8]{0:T(128)S(1)} fusion(f32[48,768]{1,0:T(8,128)S(1)} %get-tuple-element.12, bf16[8,1,48,768]{3,2,1,0:T(8,128)(2,1)} %param.11, pred[48,768]{1,0:T(8,128)(4,1)} %copy-done.3), kind=kLoop, calls=%fused_computation.6 | loop fusion | flops 1179640 | bytes 774176 | tf_op jit(solution)/shard_map/reduce_sum | solution.py:47
  46.5 0.7 pad_maximum_fusion
  47.3 33.6 %all_to_all.29 = f32[32,1,73]{2,1,0:T(1,128)S(1)} all-to-all(f32[32,1,73]{2,1,0:T(1,128)S(1)} %broadcast_in_dim.23), channel_id=1, replica_groups=mesh['ops'=16,'sec'=32] {'sec'}, dimensions={0} | all-to-all | bytes 18688 | tf_op jit(solution)/shard_map/all_to_all | solution.py:18
  80.9 9.4 %all_to_all.30 = f32[16,1,73]{2,1,0:T(1,128)S(1)} all-to-all(f32[16,1,73]{2,1,0:T(1,128)S(1)} %broadcast_in_dim.24), channel_id=1, replica_groups=mesh['ops'=16,'sec'=32] {'ops'}, dimensions={0} | all-to-all | bytes 9344 | tf_op jit(solution)/shard_map/all_to_all | solution.py:18
  90.3 0.6 slice.11
  90.9 0.1 slice.13
  91.0 0.1 slice.14
  91.0 0.2 fusion.1
  91.2 0.7 multiply_reduce_fusion.2
  93.9 0.7 divide_convert_fusion.1
  94.6 0.6 copy-done.5
  (18 shorter events, 0.1 us)
Async XLA Ops:
  0.6 1.4 %copy-start = (bf16[1,1,768,768]{3,2,1,0:T(8,128)(2,1)S(1)}, bf16[1,1,768,768]{3,2,1,0:T(8,128)(2,1)}, u32[]{:S(2)}) copy-start(bf16[1,1,768,768]{3,2,1,0:T(8,128)(2,1)} %param.9) | copy-start | bytes 3538948
  7.1 35.5 %all-to-all-start.2 = ((f32[16,48,768]{2,1,0:T(8,128)}), f32[16,48,768]{2,1,0:T(8,128)S(1)}, u32[]{:S(2)}, u32[]{:S(2)}) async-start(f32[16,48,768]{2,1,0:T(8,128)} %bitcast.42), calls=%async_computation.2 | async-start | bytes 4718592 | tf_op jit(solution)/shard_map/all_to_all | solution.py:10
  14.9 0.6 copy-start.3
  43.4 47.6 %copy-start.1 = (bf16[8,1,48,768]{3,2,1,0:T(8,128)(2,1)S(1)}, bf16[8,1,48,768]{3,2,1,0:T(8,128)(2,1)}, u32[]{:S(2)}) copy-start(bf16[8,1,48,768]{3,2,1,0:T(8,128)(2,1)} %param.11) | copy-start | bytes 1769476
  43.4 47.6 %copy-start.4 = (pred[48,768]{1,0:T(8,128)(4,1)S(1)}, pred[48,768]{1,0:T(8,128)(4,1)}, u32[]{:S(2)}) copy-start(pred[48,768]{1,0:T(8,128)(4,1)} %copy-done.3) | copy-start | bytes 110596
  43.4 50.4 %copy-start.2 = (f32[48,768]{1,0:T(8,128)S(1)}, f32[48,768]{1,0:T(8,128)}, u32[]{:S(2)}) copy-start(f32[48,768]{1,0:T(8,128)} %reduce_sum.94) | copy-start | bytes 442372
  90.3 4.3 %copy-start.6 = (f32[73]{0:T(128)}, f32[73]{0:T(128)S(1)}, u32[]{:S(2)}) copy-start(f32[73]{0:T(128)S(1)} %reduce_sum.99) | copy-start | bytes 880
  94.6 0.6 copy-start.5

commit v7 on v6

--- a/solution.py
+++ b/solution.py
@@ -8,7 +8,10 @@
     n = lax.axis_size("ops")
     blocks = partial.reshape(n, shard_rows, partial.shape[2])
     got = lax.all_to_all(blocks, "ops", 0, 0, tiled=True)
-    return jnp.sum(got, axis=0, keepdims=True)
+    acc = got[0]
+    for i in range(1, n):
+        acc = acc + got[i]
+    return acc[None]
 
 
 def small_sum(v):

time: 95.7 us -> 95.1 us (level)
  other arithmetic: 7.4 us -> 5.59 us
  local copies, waits for them, and re-layouts: 2.1 us -> 3.11 us
    reduce_sum x1, other arithmetic: 1.37 us -> 0.31 us  [shards(): local_over = jnp.sum(pmask * sig32[None], axis=(1, 2, 3))]
    reduce_sum x1, other arithmetic: 1.7 us -> 0.64 us  [shards(): sig_sq = jnp.sum(sig32 * sig32)]
    unnamed x14 -> x16, local copies, waits for them, and re-layouts: 1.26 us -> 2.2 us
where the time goes in v7:
time: 95.1 us; the launch traced here: 94.6 us
  blocking collectives  43 us (45%)
  waiting for transfers between devices  25.5 us (27%)
  starting transfers between devices  7.58 us (8%)
  matrix products  5.61 us (6%)
  other arithmetic  5.59 us (6%)
  between operations  4.23 us (4%)
  local copies, waits for them, and re-layouts  3.11 us (3%)
    all_to_all x2, blocking collectives, small_sum(): lax.all_to_all(x, ax, 0, 0, tiled=True)  43 us
    all_to_all x1, waiting for transfers between devices, reduce_rows(): got = lax.all_to_all(blocks, 'ops', 0, 0, tiled=True)  25.5 us
    all_to_all x1, starting transfers between devices, reduce_rows(): got = lax.all_to_all(blocks, 'ops', 0, 0, tiled=True)  7.58 us
    dot_general x1, matrix products, shards(): jnp.dot(left_ops[0, 0], inner, preferred_element_type=jnp.float32)[None]  5.09 us
    unnamed x16, local copies, waits for them, and re-layouts  2.2 us
  transfers between devices with their start and end apart: 1, of which 1 were waited for; matrix products, arithmetic and copies ran while one was open for 2% of the time, Pallas kernels for 0%

profile of v7, /device:TPU:1, one launch (start us, length us, event | category | flops | bytes accessed | tf_op | source)
XLA Modules:
  0.0 94.6 jit_solution(2345888858197125266)
XLA Ops:
  0.6 0.0 copy-start
  2.1 5.1 %fusion.5 = f32[768,768]{0,1:T(8,128)} fusion(bf16[1,1,768,768]{3,2,1,0:T(8,128)(2,1)S(1)} %copy-done, bf16[1,768,768]{2,1,0:T(8,128)(2,1)} %param.8, bf16[1,1,768,768]{3,2,1,0:T(8,128)(2,1)} %param.10, f32[768]{0:T(1024)S(1)} %get-tuple-element.13, f32[768]{0:T(1024)S(1)} %get-tuple-element.12), kind=kOutput, calls=%fused_computation.10 | convolution fusion | flops 1814298624 | bytes 5904384 | tf_op jit(solution)/shard_map/dot_general | solution.py:38
  7.1 7.6 %all-to-all-start.2 = ((f32[16,48,768]{2,1,0:T(8,128)}), f32[16,48,768]{2,1,0:T(8,128)S(1)}, u32[]{:S(2)}, u32[]{:S(2)}) async-start(f32[16,48,768]{2,1,0:T(8,128)} %bitcast.39), calls=%async_computation.2 | async-start | bytes 4718592 | tf_op jit(solution)/shard_map/all_to_all | solution.py:10
  14.8 0.1 broadcast_and_fusion
  14.9 0.6 copy-done.4
  15.5 1.1 %fusion.15 = bf16[8,48,768]{2,1,0:T(8,128)(2,1)S(1)} fusion(bf16[8,1,48,768]{3,2,1,0:T(8,128)(2,1)} %param.11, pred[48,768]{1,0:T(8,128)(4,1)S(1)} %broadcast_and_fusion), kind=kLoop, calls=%fused_computation.18 | loop fusion | flops 294912 | bytes 1216512 | tf_op jit(solution)/shard_map/reshape.24
  16.6 0.5 convolution_bitcast_fusion
  17.1 0.1 reshape.320
  17.2 25.5 %all-to-all-done.2 = f32[16,48,768]{2,1,0:T(8,128)S(1)} async-done(((f32[16,48,768]{2,1,0:T(8,128)}), f32[16,48,768]{2,1,0:T(8,128)S(1)}, u32[]{:S(2)}, u32[]{:S(2)}) %all-to-all-start.2) | async-done | bytes 2359328 | tf_op jit(solution)/shard_map/all_to_all | solution.py:10
  42.7 0.1 convert_bitcast_fusion
  42.8 0.0 copy-start.3
  42.8 0.9 copy-done.1
  43.8 0.3 fusion
  44.1 0.6 fusion.16
  44.7 0.7 pad_maximum_fusion
  45.5 33.6 %all_to_all.29 = f32[32,1,73]{2,1,0:T(1,128)S(1)} all-to-all(f32[32,1,73]{2,1,0:T(1,128)S(1)} %broadcast_in_dim.23), channel_id=1, replica_groups=mesh['ops'=16,'sec'=32] {'sec'}, dimensions={0} | all-to-all | bytes 18688 | tf_op jit(solution)/shard_map/all_to_all | solution.py:21
  79.1 9.4 %all_to_all.30 = f32[16,1,73]{2,1,0:T(1,128)S(1)} all-to-all(f32[16,1,73]{2,1,0:T(1,128)S(1)} %broadcast_in_dim.24), channel_id=1, replica_groups=mesh['ops'=16,'sec'=32] {'ops'}, dimensions={0} | all-to-all | bytes 9344 | tf_op jit(solution)/shard_map/all_to_all | solution.py:21
  88.5 0.1 slice.77
  88.6 0.7 slice.75
  89.2 0.9 fusion.1
  90.2 0.1 slice.78
  90.3 0.7 multiply_reduce_fusion.1
  93.0 0.9 divide_convert_fusion.1
  94.0 0.6 copy-done.6
  (20 shorter events, 0.1 us)
Async XLA Ops:
  0.6 1.4 %copy-start = (bf16[1,1,768,768]{3,2,1,0:T(8,128)(2,1)S(1)}, bf16[1,1,768,768]{3,2,1,0:T(8,128)(2,1)}, u32[]{:S(2)}) copy-start(bf16[1,1,768,768]{3,2,1,0:T(8,128)(2,1)} %param.9) | copy-start | bytes 3538948
  7.1 35.5 %all-to-all-start.2 = ((f32[16,48,768]{2,1,0:T(8,128)}), f32[16,48,768]{2,1,0:T(8,128)S(1)}, u32[]{:S(2)}, u32[]{:S(2)}) async-start(f32[16,48,768]{2,1,0:T(8,128)} %bitcast.39), calls=%async_computation.2 | async-start | bytes 4718592 | tf_op jit(solution)/shard_map/all_to_all | solution.py:10
  14.9 0.6 copy-start.4
  42.7 1.1 %copy-start.1 = (bf16[8,1,48,768]{3,2,1,0:T(8,128)(2,1)S(1)}, bf16[8,1,48,768]{3,2,1,0:T(8,128)(2,1)}, u32[]{:S(2)}) copy-start(bf16[8,1,48,768]{3,2,1,0:T(8,128)(2,1)} %param.11) | copy-start | bytes 1769476
  42.7 1.1 %copy-start.5 = (pred[48,768]{1,0:T(8,128)(4,1)S(1)}, pred[48,768]{1,0:T(8,128)(4,1)}, u32[]{:S(2)}) copy-start(pred[48,768]{1,0:T(8,128)(4,1)} %copy-done.4) | copy-start | bytes 110596
  42.8 1.3 %copy-start.3 = (bf16[1,48,768]{2,1,0:T(8,128)(2,1)}, bf16[1,48,768]{2,1,0:T(8,128)(2,1)S(1)}, u32[]{:S(2)}) copy-start(bf16[1,48,768]{2,1,0:T(8,128)(2,1)S(1)} %get-tuple-element.11) | copy-start | bytes 221188
  42.8 46.4 %copy-start.2 = (bf16[8,1,48,768]{3,2,1,0:T(8,128)(2,1)S(1)}, bf16[8,1,48,768]{3,2,1,0:T(8,128)(2,1)}, u32[]{:S(2)}) copy-start(bf16[8,1,48,768]{3,2,1,0:T(8,128)(2,1)} %param.11) | copy-start | bytes 1769476
  88.5 5.5 %copy-start.7 = (f32[73]{0:T(128)}, f32[73]{0:T(128)S(1)}, u32[]{:S(2)}) copy-start(f32[73]{0:T(128)S(1)} %reduce_sum.86) | copy-start | bytes 880
  93.9 0.6 copy-start.6

commit v8 on v7

--- a/solution.py
+++ b/solution.py
@@ -57,7 +57,9 @@
     sig_sq_all = sums[-1]
     resid = sig32 - jnp.sum(correlations[:, None, None, None] * pmask, axis=0)
     eye = jnp.eye(nprior, dtype=jnp.float32)
-    expanded = sig_sq_all + jnp.sum(correlations[:, None] * correlations[None, :] * (gram_all - 2.0 * eye))
+    expanded = sig_sq_all + jnp.sum(
+        correlations[:, None] * correlations[None, :] * (gram_all - 2.0 * eye), keepdims=True
+    )
     cells = sec_local * lax.axis_size("sec") * width * width
 
     def scaled(total):
@@ -65,9 +67,9 @@
 
     fast = scaled(expanded)
     new_dir = lax.cond(
-        expanded >= sig_sq_all * 0.0625,
+        expanded[0, 0] >= sig_sq_all * 0.0625,
         lambda r: fast,
-        lambda r: scaled(small_sum(jnp.sum(r * r))),
+        lambda r: scaled(small_sum(jnp.sum(r * r, keepdims=True))),
         resid,
     )
     return (sigma, new_dir, correlations)

time: 95.1 us -> 94.7 us (level)
  no operation moved by 1% of the time
where the time goes in v8:
time: 94.7 us; the launch traced here: 94.2 us
  blocking collectives  43 us (45%)
  waiting for transfers between devices  25.5 us (27%)
  starting transfers between devices  7.58 us (8%)
  matrix products  5.61 us (6%)
  other arithmetic  5.59 us (6%)
  between operations  3.97 us (4%)
  local copies, waits for them, and re-layouts  3.02 us (3%)
    all_to_all x2, blocking collectives, small_sum(): lax.all_to_all(x, ax, 0, 0, tiled=True)  43 us
    all_to_all x1, waiting for transfers between devices, reduce_rows(): got = lax.all_to_all(blocks, 'ops', 0, 0, tiled=True)  25.5 us
    all_to_all x1, starting transfers between devices, reduce_rows(): got = lax.all_to_all(blocks, 'ops', 0, 0, tiled=True)  7.58 us
    dot_general x1, matrix products, shards(): jnp.dot(left_ops[0, 0], inner, preferred_element_type=jnp.float32)[None]  5.09 us
    unnamed x16, local copies, waits for them, and re-layouts  2.2 us
  transfers between devices with their start and end apart: 1, of which 1 were waited for; matrix products, arithmetic and copies ran while one was open for 2% of the time, Pallas kernels for 0%

profile of v8, /device:TPU:1, one launch (start us, length us, event | category | flops | bytes accessed | tf_op | source)
XLA Modules:
  0.0 94.2 jit_solution(13309584681554008674)
XLA Ops:
  0.6 0.0 copy-start
  2.1 5.1 %fusion.5 = f32[768,768]{0,1:T(8,128)} fusion(bf16[1,1,768,768]{3,2,1,0:T(8,128)(2,1)S(1)} %copy-done, bf16[1,768,768]{2,1,0:T(8,128)(2,1)} %param.8, bf16[1,1,768,768]{3,2,1,0:T(8,128)(2,1)} %param.10, f32[768]{0:T(1024)S(1)} %get-tuple-element.13, f32[768]{0:T(1024)S(1)} %get-tuple-element.12), kind=kOutput, calls=%fused_computation.10 | convolution fusion | flops 1814298624 | bytes 5904384 | tf_op jit(solution)/shard_map/dot_general | solution.py:38
  7.1 7.6 %all-to-all-start.2 = ((f32[16,48,768]{2,1,0:T(8,128)}), f32[16,48,768]{2,1,0:T(8,128)S(1)}, u32[]{:S(2)}, u32[]{:S(2)}) async-start(f32[16,48,768]{2,1,0:T(8,128)} %bitcast.43), calls=%async_computation.2 | async-start | bytes 4718592 | tf_op jit(solution)/shard_map/all_to_all | solution.py:10
  14.8 0.1 broadcast_and_fusion
  14.9 0.6 copy-done.4
  15.5 1.1 %fusion.15 = bf16[8,48,768]{2,1,0:T(8,128)(2,1)S(1)} fusion(bf16[8,1,48,768]{3,2,1,0:T(8,128)(2,1)} %param.11, pred[48,768]{1,0:T(8,128)(4,1)S(1)} %broadcast_and_fusion), kind=kLoop, calls=%fused_computation.18 | loop fusion | flops 294912 | bytes 1216512 | tf_op jit(solution)/shard_map/reshape.24
  16.6 0.5 convolution_bitcast_fusion
  17.1 0.1 reshape.332
  17.2 25.5 %all-to-all-done.2 = f32[16,48,768]{2,1,0:T(8,128)S(1)} async-done(((f32[16,48,768]{2,1,0:T(8,128)}), f32[16,48,768]{2,1,0:T(8,128)S(1)}, u32[]{:S(2)}, u32[]{:S(2)}) %all-to-all-start.2) | async-done | bytes 2359328 | tf_op jit(solution)/shard_map/all_to_all | solution.py:10
  42.7 0.1 convert_bitcast_fusion
  42.8 0.0 copy-start.3
  42.8 0.9 copy-done.1
  43.8 0.3 fusion
  44.1 0.6 fusion.16
  44.7 0.7 pad_maximum_fusion
  45.5 33.6 %all_to_all.29 = f32[32,1,73]{2,1,0:T(1,128)S(1)} all-to-all(f32[32,1,73]{2,1,0:T(1,128)S(1)} %broadcast_in_dim.25), channel_id=1, replica_groups=mesh['ops'=16,'sec'=32] {'sec'}, dimensions={0} | all-to-all | bytes 18688 | tf_op jit(solution)/shard_map/all_to_all | solution.py:21
  79.1 9.4 %all_to_all.30 = f32[16,1,73]{2,1,0:T(1,128)S(1)} all-to-all(f32[16,1,73]{2,1,0:T(1,128)S(1)} %broadcast_in_dim.26), channel_id=1, replica_groups=mesh['ops'=16,'sec'=32] {'ops'}, dimensions={0} | all-to-all | bytes 9344 | tf_op jit(solution)/shard_map/all_to_all | solution.py:21
  88.5 0.1 slice.77
  88.6 0.6 slice.75
  89.1 0.1 slice.78
  89.2 1.0 %fusion.1 = f32[48,768]{1,0:T(8,128)S(1)} fusion(f32[8]{0:T(128)S(1)} %bitcast.46, bf16[8,1,48,768]{3,2,1,0:T(8,128)(2,1)S(1)} %copy-done.2, pred[48,768]{1,0:T(8,128)(4,1)} %copy-done.4), kind=kLoop, calls=%fused_computation.7 | loop fusion | flops 1142784 | bytes 774176 | tf_op jit(solution)/shard_map/reduce_sum | solution.py:58
  90.2 0.7 multiply_reduce_fusion.1
  92.7 0.9 divide_convert_fusion.1
  93.6 0.6 copy-done.6
  (20 shorter events, 0.1 us)
Async XLA Ops:
  0.6 1.4 %copy-start = (bf16[1,1,768,768]{3,2,1,0:T(8,128)(2,1)S(1)}, bf16[1,1,768,768]{3,2,1,0:T(8,128)(2,1)}, u32[]{:S(2)}) copy-start(bf16[1,1,768,768]{3,2,1,0:T(8,128)(2,1)} %param.9) | copy-start | bytes 3538948
  7.1 35.5 %all-to-all-start.2 = ((f32[16,48,768]{2,1,0:T(8,128)}), f32[16,48,768]{2,1,0:T(8,128)S(1)}, u32[]{:S(2)}, u32[]{:S(2)}) async-start(f32[16,48,768]{2,1,0:T(8,128)} %bitcast.43), calls=%async_computation.2 | async-start | bytes 4718592 | tf_op jit(solution)/shard_map/all_to_all | solution.py:10
  14.9 0.6 copy-start.4
  42.7 1.1 %copy-start.1 = (bf16[8,1,48,768]{3,2,1,0:T(8,128)(2,1)S(1)}, bf16[8,1,48,768]{3,2,1,0:T(8,128)(2,1)}, u32[]{:S(2)}) copy-start(bf16[8,1,48,768]{3,2,1,0:T(8,128)(2,1)} %param.11) | copy-start | bytes 1769476
  42.7 1.1 %copy-start.5 = (pred[48,768]{1,0:T(8,128)(4,1)S(1)}, pred[48,768]{1,0:T(8,128)(4,1)}, u32[]{:S(2)}) copy-start(pred[48,768]{1,0:T(8,128)(4,1)} %copy-done.4) | copy-start | bytes 110596
  42.8 1.3 %copy-start.3 = (bf16[1,48,768]{2,1,0:T(8,128)(2,1)}, bf16[1,48,768]{2,1,0:T(8,128)(2,1)S(1)}, u32[]{:S(2)}) copy-start(bf16[1,48,768]{2,1,0:T(8,128)(2,1)S(1)} %get-tuple-element.11) | copy-start | bytes 221188
  42.8 46.4 %copy-start.2 = (bf16[8,1,48,768]{3,2,1,0:T(8,128)(2,1)S(1)}, bf16[8,1,48,768]{3,2,1,0:T(8,128)(2,1)}, u32[]{:S(2)}) copy-start(bf16[8,1,48,768]{3,2,1,0:T(8,128)(2,1)} %param.11) | copy-start | bytes 1769476
  88.5 5.1 %copy-start.7 = (f32[73]{0:T(128)}, f32[73]{0:T(128)S(1)}, u32[]{:S(2)}) copy-start(f32[73]{0:T(128)S(1)} %reduce_sum.86) | copy-start | bytes 880
  93.6 0.6 copy-start.6

commit v9 on v8

--- a/solution.py
+++ b/solution.py
@@ -47,14 +47,13 @@
     gram = jnp.einsum("psab,qsab->pq", pmask, pmask, precision=lax.Precision.HIGHEST)
     sigma = (summed * mine_mask).astype(jnp.bfloat16)
     sig32 = sigma.astype(jnp.float32)
-    local_over = jnp.sum(pmask * sig32[None], axis=(1, 2, 3))
-    sig_sq = jnp.sum(sig32 * sig32)
-    nprior = local_over.shape[0]
-    packed = jnp.concatenate([local_over, gram.reshape(-1), sig_sq[None]])
+    stats = jnp.sum(jnp.concatenate([pmask, sig32[None]], axis=0) * sig32[None], axis=(1, 2, 3))
+    nprior = pmask.shape[0]
+    packed = jnp.concatenate([stats, gram.reshape(-1)])
     sums = small_sum(packed)
     correlations = sums[:nprior]
-    gram_all = sums[nprior:-1].reshape(nprior, nprior)
-    sig_sq_all = sums[-1]
+    sig_sq_all = sums[nprior]
+    gram_all = sums[nprior + 1:].reshape(nprior, nprior)
     resid = sig32 - jnp.sum(correlations[:, None, None, None] * pmask, axis=0)
     eye = jnp.eye(nprior, dtype=jnp.float32)
     expanded = sig_sq_all + jnp.sum(

time: 94.7 us -> 92.8 us (0.980)
  other arithmetic: 5.59 us -> 4.55 us
    convert_element_type x0 -> x1, other arithmetic: none -> 2.21 us  [shards(): jnp.where(prior_ok[None], priors, jnp.zeros_like(priors))]
    another operation x1 -> x0, other arithmetic: 1.11 us -> none
  transfers between devices with their start and end apart: 1 -> 1, of which waited for: 1 -> 1; matrix products, arithmetic and copies ran while one was open for 2% -> 3% of each run, Pallas kernels for 0% -> 0%
where the time goes in v9:
time: 92.8 us; the launch traced here: 92.4 us
  blocking collectives  43.1 us (46%)
  waiting for transfers between devices  25 us (27%)
  starting transfers between devices  7.57 us (8%)
  matrix products  5.61 us (6%)
  other arithmetic  4.55 us (5%)
  between operations  3.99 us (4%)
  local copies, waits for them, and re-layouts  2.6 us (3%)
    all_to_all x2, blocking collectives, small_sum(): lax.all_to_all(x, ax, 0, 0, tiled=True)  43.1 us
    all_to_all x1, waiting for transfers between devices, reduce_rows(): got = lax.all_to_all(blocks, 'ops', 0, 0, tiled=True)  25 us
    all_to_all x1, starting transfers between devices, reduce_rows(): got = lax.all_to_all(blocks, 'ops', 0, 0, tiled=True)  7.57 us
    dot_general x1, matrix products, shards(): jnp.dot(left_ops[0, 0], inner, preferred_element_type=jnp.float32)[None]  5.09 us
    convert_element_type x1, other arithmetic, shards(): jnp.where(prior_ok[None], priors, jnp.zeros_like(priors))  2.21 us
  transfers between devices with their start and end apart: 1, of which 1 were waited for; matrix products, arithmetic and copies ran while one was open for 3% of the time, Pallas kernels for 0%

profile of v9, /device:TPU:1, one launch (start us, length us, event | category | flops | bytes accessed | tf_op | source)
XLA Modules:
  0.0 92.4 jit_solution(11034685111720243087)
XLA Ops:
  0.6 0.0 copy-start
  2.1 5.1 %fusion.4 = f32[768,768]{0,1:T(8,128)} fusion(bf16[1,1,768,768]{3,2,1,0:T(8,128)(2,1)S(1)} %copy-done, bf16[1,768,768]{2,1,0:T(8,128)(2,1)} %param.8, bf16[1,1,768,768]{3,2,1,0:T(8,128)(2,1)} %param.10, f32[768]{0:T(1024)S(1)} %get-tuple-element.15, f32[768]{0:T(1024)S(1)} %fusion.18), kind=kOutput, calls=%fused_computation.8 | convolution fusion | flops 1814298624 | bytes 5904384 | tf_op jit(solution)/shard_map/dot_general | solution.py:38
  7.2 7.6 %all-to-all-start.2 = ((f32[16,48,768]{2,1,0:T(8,128)}), f32[16,48,768]{2,1,0:T(8,128)S(1)}, u32[]{:S(2)}, u32[]{:S(2)}) async-start(f32[16,48,768]{2,1,0:T(8,128)} %bitcast.43), calls=%async_computation.2 | async-start | bytes 4718592 | tf_op jit(solution)/shard_map/all_to_all | solution.py:10
  14.8 0.1 broadcast_and_fusion
  14.8 0.0 copy-start.4
  14.9 2.2 %fusion.15 = (f32[8,1,48,768]{3,2,1,0:T(8,128)}, bf16[8,48,768]{2,1,0:T(8,128)(2,1)S(1)}) fusion(bf16[8,1,48,768]{3,2,1,0:T(8,128)(2,1)} %param.11, pred[48,768]{1,0:T(8,128)(4,1)S(1)} %broadcast_and_fusion), kind=kLoop, calls=%fused_computation.18 | loop fusion | flops 589824 | bytes 2396160 | tf_op jit(solution)/shard_map/convert_element_type | solution.py:46
  17.1 0.5 convolution_bitcast_fusion
  17.6 0.1 reshape.351
  17.7 25.0 %all-to-all-done.2 = f32[16,48,768]{2,1,0:T(8,128)S(1)} async-done(((f32[16,48,768]{2,1,0:T(8,128)}), f32[16,48,768]{2,1,0:T(8,128)S(1)}, u32[]{:S(2)}, u32[]{:S(2)}) %all-to-all-start.2) | async-done | bytes 2359328 | tf_op jit(solution)/shard_map/all_to_all | solution.py:10
  42.7 0.1 convert_bitcast_fusion
  42.8 0.0 copy-start.3
  42.8 0.0 copy-start.5
  42.8 1.1 %copy-done.1 = f32[8,1,48,768]{3,2,1,0:T(8,128)S(1)} copy-done((f32[8,1,48,768]{3,2,1,0:T(8,128)S(1)}, f32[8,1,48,768]{3,2,1,0:T(8,128)}, u32[]{:S(2)}) %copy-start.1) | copy-done | bytes 1179672
  44.0 0.2 fusion
  44.2 0.1 pad_maximum_fusion
  44.3 33.7 %all_to_all.29 = f32[32,1,73]{2,1,0:T(1,128)S(1)} all-to-all(f32[32,1,73]{2,1,0:T(1,128)S(1)} %broadcast_in_dim.22), channel_id=1, replica_groups=mesh['ops'=16,'sec'=32] {'sec'}, dimensions={0} | all-to-all | bytes 18688 | tf_op jit(solution)/shard_map/all_to_all | solution.py:21
  78.0 9.4 %all_to_all.30 = f32[16,1,73]{2,1,0:T(1,128)S(1)} all-to-all(f32[16,1,73]{2,1,0:T(1,128)S(1)} %broadcast_in_dim.23), channel_id=1, replica_groups=mesh['ops'=16,'sec'=32] {'ops'}, dimensions={0} | all-to-all | bytes 9344 | tf_op jit(solution)/shard_map/all_to_all | solution.py:21
  87.4 0.1 slice.77
  87.5 0.6 slice.75
  88.0 0.1 slice.78
  88.1 0.2 multiply_reduce_fusion.1
  88.3 0.7 multiply_reduce_fusion.2
  90.8 0.9 divide_convert_fusion.1
  91.7 0.6 copy-done.6
  (20 shorter events, 0.1 us)
Async XLA Ops:
  0.6 1.4 %copy-start = (bf16[1,1,768,768]{3,2,1,0:T(8,128)(2,1)S(1)}, bf16[1,1,768,768]{3,2,1,0:T(8,128)(2,1)}, u32[]{:S(2)}) copy-start(bf16[1,1,768,768]{3,2,1,0:T(8,128)(2,1)} %param.9) | copy-start | bytes 3538948
  7.2 35.5 %all-to-all-start.2 = ((f32[16,48,768]{2,1,0:T(8,128)}), f32[16,48,768]{2,1,0:T(8,128)S(1)}, u32[]{:S(2)}, u32[]{:S(2)}) async-start(f32[16,48,768]{2,1,0:T(8,128)} %bitcast.43), calls=%async_computation.2 | async-start | bytes 4718592 | tf_op jit(solution)/shard_map/all_to_all | solution.py:10
  14.8 2.2 %copy-start.4 = (pred[48,768]{1,0:T(8,128)(4,1)}, pred[48,768]{1,0:T(8,128)(4,1)S(1)}, u32[]{:S(2)}) copy-start(pred[48,768]{1,0:T(8,128)(4,1)S(1)} %broadcast_and_fusion) | copy-start | bytes 110596
  42.7 1.3 %copy-start.1 = (f32[8,1,48,768]{3,2,1,0:T(8,128)S(1)}, f32[8,1,48,768]{3,2,1,0:T(8,128)}, u32[]{:S(2)}) copy-start(f32[8,1,48,768]{3,2,1,0:T(8,128)} %get-tuple-element.12) | copy-start | bytes 3538948
  42.8 1.4 %copy-start.3 = (bf16[1,48,768]{2,1,0:T(8,128)(2,1)}, bf16[1,48,768]{2,1,0:T(8,128)(2,1)S(1)}, u32[]{:S(2)}) copy-start(bf16[1,48,768]{2,1,0:T(8,128)(2,1)S(1)} %get-tuple-element.11) | copy-start | bytes 221188
  42.8 45.3 %copy-start.2 = (bf16[8,1,48,768]{3,2,1,0:T(8,128)(2,1)S(1)}, bf16[8,1,48,768]{3,2,1,0:T(8,128)(2,1)}, u32[]{:S(2)}) copy-start(bf16[8,1,48,768]{3,2,1,0:T(8,128)(2,1)} %param.11) | copy-start | bytes 1769476
  42.8 45.3 %copy-start.5 = (pred[48,768]{1,0:T(8,128)(4,1)S(1)}, pred[48,768]{1,0:T(8,128)(4,1)}, u32[]{:S(2)}) copy-start(pred[48,768]{1,0:T(8,128)(4,1)} %copy-done.4) | copy-start | bytes 110596
  87.4 4.3 %copy-start.7 = (f32[73]{0:T(128)}, f32[73]{0:T(128)S(1)}, u32[]{:S(2)}) copy-start(f32[73]{0:T(128)S(1)} %reduce_sum.76) | copy-start | bytes 880
  91.7 0.6 copy-start.6
